TPU v7x, 1024 devices: a whole 4x4x32 slice. The times are simulated.
1024 devices in a mesh: expert: 64 (over z, core), mp: 16 (over y, x).
Axes of the slice: x: 4, y: 4, z: 32, core: 2. Of those that a mesh axis runs over, the one named last changes fastest.
Arguments:
- tokens: bfloat16 [8192, 4096], P('expert', 'mp'), may hold values from -6 to 6
- expert_ids: int32 [8192, 1], P('expert'), may hold values from 0 to 63; in each aligned block of 128 rows (0 to 127, 128 to 255, ...) at most 4 rows name the same one
- seq_lengths: int32 [64], P('expert'), may hold values from 64 to 128, as said below
- hidden_cotangent: bfloat16 [64, 256, 6144], P('expert', None, 'mp'), may hold values from -6 to 6
- w_in: bfloat16 [64, 4096, 6144], P('expert', None, 'mp'), may hold values from -0.09375 to 0.09375
Outputs:
- grad_tokens: bfloat16 [8192, 4096], P('expert', 'mp')
Inputs may be any that keep to these rules, and one draw needn't show every extreme that they name: `expert_ids`: in each aligned block of 128 rows no expert is named by more than 4 rows, a bound that some block reaches. `seq_lengths`: some sequence is full and some has exactly 64 live positions.
All inputs are finite; a program needn't handle non-finite values.
Results may differ from a plain program's by a relative error of at most 0.014.
Values may be sent and summed in bfloat16 or wider, within the bound.
No kernel may reach another device: no remote copies, remote signals or barrier semaphores. Data moves between devices by JAX's collectives and lax.ppermute only.
A program may use at most 32 MiB of HBM per device.

v0:
```python
import math

import jax
import jax.numpy as jnp
from jax import lax
from jax.sharding import PartitionSpec as P

SEQ_LEN = 128


def gelu_slope(preact):
    coeff = math.sqrt(2.0 / math.pi)
    squashed = jnp.tanh(coeff * (preact + 0.044715 * preact * preact * preact))
    return 0.5 * (1.0 + squashed) + 0.5 * preact * (1.0 - squashed * squashed) * coeff * (
        1.0 + 3.0 * 0.044715 * preact * preact
    )


def per_device(tokens, expert_ids, seq_lengths, hidden_cotangent, w_in):
    tok_dev = tokens.shape[0]
    experts = w_in.shape[0] * lax.axis_size("expert")
    capacity = max(2, 2 * tok_dev // experts)
    position = jnp.arange(tok_dev, dtype=jnp.int32)
    seq_index = position // SEQ_LEN
    seq_length = jnp.sum(
        jnp.where(
            seq_index[:, None] == jnp.arange(seq_lengths.shape[0], dtype=jnp.int32)[None, :],
            seq_lengths[None, :],
            0,
        ),
        axis=1,
    )
    live_mask = position % SEQ_LEN < seq_length
    expert_row = expert_ids[:, 0]
    onehot = (
        (expert_row[:, None] == jnp.arange(experts, dtype=jnp.int32)[None, :]) & live_mask[:, None]
    ).astype(jnp.int32)
    slot_rank = jnp.sum(jnp.cumsum(onehot, axis=0) * onehot, axis=1) - 1
    target = jnp.where(live_mask, expert_row * capacity + slot_rank, experts * capacity)
    buffer = (
        jnp.zeros((experts * capacity + 1,) + tokens.shape[1:], tokens.dtype).at[target].set(tokens)
    )
    arrived = lax.all_to_all(
        buffer[:-1].reshape((experts, capacity) + tokens.shape[1:]),
        "expert",
        split_axis=0,
        concat_axis=0,
        tiled=True,
    )
    slot_count = arrived.shape[0] * capacity
    features = lax.all_gather(
        arrived.reshape(slot_count, arrived.shape[2]), "mp", axis=1, tiled=True
    )
    weight = w_in[0]
    pre_act = jnp.dot(features, weight, preferred_element_type=jnp.float32)
    hidden_grad = (hidden_cotangent[0].astype(jnp.float32) * gelu_slope(pre_act)).astype(
        jnp.bfloat16
    )
    partial_value = lax.dot_general(
        hidden_grad, weight, (((1,), (1,)), ((), ())), preferred_element_type=jnp.float32
    ).astype(jnp.bfloat16)
    partial_value = lax.optimization_barrier(partial_value)
    summed = lax.psum_scatter(
        partial_value.astype(jnp.float32).astype(jnp.bfloat16),
        "mp",
        scatter_dimension=1,
        tiled=True,
    )
    returned = lax.all_to_all(
        summed.reshape(arrived.shape[0], capacity, summed.shape[1]),
        "expert",
        split_axis=0,
        concat_axis=0,
        tiled=True,
    )
    flat_rows = returned.reshape((experts * capacity,) + returned.shape[2:])
    padded = jnp.concatenate(
        [flat_rows, jnp.zeros((1,) + flat_rows.shape[1:], flat_rows.dtype)], axis=0
    )
    return padded[target]


def solution(mesh):
    in_specs = (
        P("expert", "mp"),
        P("expert", None),
        P("expert"),
        P("expert", None, "mp"),
        P("expert", None, "mp"),
    )
    out_specs = P("expert", "mp")
    return jax.shard_map(
        per_device, mesh=mesh, in_specs=in_specs, out_specs=out_specs, check_vma=False
    )
```

profile of v0, /device:TPU:1, one launch (start us, length us, event | category | flops | bytes accessed | tf_op | source)
XLA Modules:
  0.0 318.7 jit_solution(1777422632792645834)
XLA Ops:
  6.5 0.0 copy-start
  6.5 0.0 all-gather.2.cloned.1.call-start
  7.4 0.9 fusion.23
  8.3 0.2 reduce_window_sum.11
  8.4 0.8 select_reduce_fusion
  9.3 0.7 fusion.25
  9.9 1.3 scatter_custom_fusion
  11.3 60.9 %all_to_all.10 = bf16[64,4,256]{2,1,0:T(4,128)(2,1)S(1)} all-to-all(bf16[64,4,256]{2,1,0:T(4,128)(2,1)S(1)} %reshape.90), channel_id=1, replica_groups=mesh['expert'=64,'mp'=16] {'expert'}, dimensions={0} | all-to-all | bytes 262144 | tf_op jit(solution)/shard_map/all_to_all | solution.py:43
  72.2 0.7 reshape.91
  72.9 0.0 all-gather.2.cloned.1.call-update
  72.9 0.0 reduce-scatter.2.cloned.1.call-start
  73.0 64.9 %all-gather.2.cloned.1.call-done = bf16[256,4096]{1,0:T(8,128)(2,1)} async-done(((bf16[256,256]{1,0:T(8,128)(2,1)}), bf16[256,4096]{1,0:T(8,128)(2,1)}) %all-gather.2.cloned.1.call-update) | async-done | bytes 2097168 | tf_op jit(solution)/shard_map/all_gather | solution.py:51
  137.9 0.0 copy-done
  137.9 5.5 %convolution_convert_fusion = bf16[256,4096]{1,0:T(8,128)(2,1)} fusion(bf16[1,4096,384]{2,1,0:T(8,128)(2,1)S(1)} %copy-done, bf16[256,4096]{1,0:T(8,128)(2,1)} %all-gather.2.cloned.1.call-done, bf16[1,256,384]{2,1,0:T(8,128)(2,1)} %param.8), kind=kOutput, calls=%fused_computation.2 | convolution fusion | flops 1613627392 | bytes 7536640 | tf_op jit(solution)/shard_map/dot_general | solution.py:59
  143.4 0.0 reduce-scatter.2.cloned.1.call-update
  143.5 109.2 %reduce-scatter.2.cloned.1.call-done = bf16[256,256]{1,0:T(8,128)(2,1)} async-done(((bf16[256,4096]{1,0:T(8,128)(2,1)}), bf16[256,256]{1,0:T(8,128)(2,1)}) %reduce-scatter.2.cloned.1.call-update) | async-done | bytes 131088 | tf_op jit(solution)/shard_map/reduce_scatter | solution.py:63
  252.6 1.6 reshape.92
  254.2 25.4 %all-to-all-start.1 = ((bf16[64,4,256]{2,1,0:T(4,128)(2,1)}), bf16[64,4,256]{2,1,0:T(4,128)(2,1)S(1)}, u32[]{:S(2)}, u32[]{:S(2)}) async-start(bf16[64,4,256]{2,1,0:T(4,128)(2,1)} %reshape.92), calls=%async_computation.2 | async-start | bytes 262144 | tf_op jit(solution)/shard_map/all_to_all | solution.py:69
  279.7 30.7 %all-to-all-done.1 = bf16[64,4,256]{2,1,0:T(4,128)(2,1)S(1)} async-done(((bf16[64,4,256]{2,1,0:T(4,128)(2,1)}), bf16[64,4,256]{2,1,0:T(4,128)(2,1)S(1)}, u32[]{:S(2)}, u32[]{:S(2)}) %all-to-all-start.1) | async-done | bytes 131104 | tf_op jit(solution)/shard_map/all_to_all | solution.py:69
  310.4 1.5 gather_fusion
  (6 shorter events, 0.1 us)
Async XLA Ops:
  6.5 131.4 %copy-start = (bf16[1,4096,384]{2,1,0:T(8,128)(2,1)S(1)}, bf16[1,4096,384]{2,1,0:T(8,128)(2,1)}, u32[]{:S(2)}) copy-start(bf16[1,4096,384]{2,1,0:T(8,128)(2,1)} %param.9) | copy-start | bytes 9437188
  6.5 131.4 %all-gather.2.cloned.1.call-start = ((), (), s32[]{:S(2)}) async-start(), calls=%async_computation.3 | async-start | bytes 2228224 | tf_op jit(solution)/shard_map/all_gather | solution.py:51
  72.9 179.7 %reduce-scatter.2.cloned.1.call-start = ((), (), s32[]{:S(2)}) async-start(), calls=%async_computation.4 | async-start | bytes 2228224 | tf_op jit(solution)/shard_map/reduce_scatter | solution.py:63
  254.2 56.1 %all-to-all-start.1 = ((bf16[64,4,256]{2,1,0:T(4,128)(2,1)}), bf16[64,4,256]{2,1,0:T(4,128)(2,1)S(1)}, u32[]{:S(2)}, u32[]{:S(2)}) async-start(bf16[64,4,256]{2,1,0:T(4,128)(2,1)} %reshape.92), calls=%async_computation.2 | async-start | bytes 262144 | tf_op jit(solution)/shard_map/all_to_all | solution.py:69
Sparse Core Ops, SparseCore 0:
  73.1 64.8 all-gather.1
  143.6 108.9 reduce-scatter.1
where the time goes:
time: 319 us
  waiting for transfers between devices  205 us (64%)
  blocking collectives  60.9 us (19%)
  starting transfers between devices  25.5 us (8%)
  between operations  14.3 us (4%)
  matrix products  5.5 us (2%)
  local copies, waits for them, and re-layouts  5.2 us (2%)
    reduce_scatter x1, waiting for transfers between devices, per_device(): lax.psum_scatter(partial_value.astype(jnp.float32).astype(jnp.bfloat16),...  109 us
    all_gather x1, waiting for transfers between devices, per_device(): lax.all_gather(arrived.reshape(slot_count, arrived.shape[2]), 'mp', axis=...  64.9 us
    all_to_all x1, blocking collectives, per_device(): lax.all_to_all(buffer[:-1].reshape((experts, capacity) + tokens.shape[1:]...  60.9 us
    all_to_all x1, waiting for transfers between devices, per_device(): lax.all_to_all(summed.reshape(arrived.shape[0], capacity, summed.shape[1]...  30.7 us
    all_to_all x1, starting transfers between devices, per_device(): lax.all_to_all(summed.reshape(arrived.shape[0], capacity, summed.shape[1]...  25.4 us
  transfers between devices with their start and end apart: 3, of which 3 were waited for; matrix products, arithmetic and copies ran while one was open for 0% of the time, Pallas kernels for 0%

commit v1 on v0

--- a/solution.py
+++ b/solution.py
@@ -14,6 +14,53 @@
     return 0.5 * (1.0 + squashed) + 0.5 * preact * (1.0 - squashed * squashed) * coeff * (
         1.0 + 3.0 * 0.044715 * preact * preact
     )
+
+
+def mp_grid():
+    n_mp = lax.axis_size("mp")
+    nx = math.isqrt(n_mp)
+    return n_mp, nx, n_mp // nx
+
+
+def shift_x(shift):
+    n_mp, nx, ny = mp_grid()
+    return [(y * nx + x, y * nx + (x + shift) % nx) for y in range(ny) for x in range(nx)]
+
+
+def shift_y(shift):
+    n_mp, nx, ny = mp_grid()
+    return [(y * nx + x, ((y + shift) % ny) * nx + x) for y in range(ny) for x in range(nx)]
+
+
+def gather_mp(block):
+    n_mp, nx, ny = mp_grid()
+    me = lax.axis_index("mp")
+    my_y, my_x = me // nx, me % nx
+    with jax.named_scope("gather_along_x"):
+        pieces = [block] + [lax.ppermute(block, "mp", shift_x(s)) for s in range(1, nx)]
+        along_x = jnp.take(jnp.stack(pieces), (my_x - jnp.arange(nx)) % nx, axis=0)
+    with jax.named_scope("gather_along_y"):
+        pieces = [along_x] + [lax.ppermute(along_x, "mp", shift_y(s)) for s in range(1, ny)]
+        full = jnp.take(jnp.stack(pieces), (my_y - jnp.arange(ny)) % ny, axis=0)
+    return full.reshape((n_mp,) + block.shape)
+
+
+def reduce_scatter_mp(parts):
+    n_mp, nx, ny = mp_grid()
+    me = lax.axis_index("mp")
+    my_y, my_x = me // nx, me % nx
+    grouped = parts.reshape((ny, nx) + parts.shape[1:])
+    with jax.named_scope("reduce_along_y"):
+        acc = lax.dynamic_index_in_dim(grouped, my_y, 0, keepdims=False).astype(jnp.float32)
+        for s in range(1, ny):
+            send = lax.dynamic_index_in_dim(grouped, (my_y + s) % ny, 0, keepdims=False)
+            acc = acc + lax.ppermute(send, "mp", shift_y(s)).astype(jnp.float32)
+    with jax.named_scope("reduce_along_x"):
+        total = lax.dynamic_index_in_dim(acc, my_x, 0, keepdims=False)
+        for s in range(1, nx):
+            send = lax.dynamic_index_in_dim(acc, (my_x + s) % nx, 0, keepdims=False)
+            total = total + lax.ppermute(send, "mp", shift_x(s))
+    return total
 
 
 def per_device(tokens, expert_ids, seq_lengths, hidden_cotangent, w_in):
@@ -48,24 +95,20 @@
         tiled=True,
     )
     slot_count = arrived.shape[0] * capacity
-    features = lax.all_gather(
-        arrived.reshape(slot_count, arrived.shape[2]), "mp", axis=1, tiled=True
+    n_mp = lax.axis_size("mp")
+    blocks = gather_mp(arrived.reshape(slot_count, arrived.shape[2]))
+    weight = w_in[0]
+    weight_blocks = weight.reshape((n_mp, weight.shape[0] // n_mp, weight.shape[1]))
+    pre_act = jnp.einsum(
+        "jsk,jkf->sf", blocks, weight_blocks, preferred_element_type=jnp.float32
     )
-    weight = w_in[0]
-    pre_act = jnp.dot(features, weight, preferred_element_type=jnp.float32)
     hidden_grad = (hidden_cotangent[0].astype(jnp.float32) * gelu_slope(pre_act)).astype(
         jnp.bfloat16
     )
-    partial_value = lax.dot_general(
-        hidden_grad, weight, (((1,), (1,)), ((), ())), preferred_element_type=jnp.float32
+    block_parts = jnp.einsum(
+        "sf,jkf->jsk", hidden_grad, weight_blocks, preferred_element_type=jnp.float32
     ).astype(jnp.bfloat16)
-    partial_value = lax.optimization_barrier(partial_value)
-    summed = lax.psum_scatter(
-        partial_value.astype(jnp.float32).astype(jnp.bfloat16),
-        "mp",
-        scatter_dimension=1,
-        tiled=True,
-    )
+    summed = reduce_scatter_mp(block_parts).astype(jnp.bfloat16)
     returned = lax.all_to_all(
         summed.reshape(arrived.shape[0], capacity, summed.shape[1]),
         "expert",

time: 319 us -> 230 us (0.72)
  waiting for transfers between devices: 205 us -> 106 us
  blocking collectives: 60.9 us -> 0 us
  starting transfers between devices: 25.5 us -> 82.2 us
  other arithmetic: 2.58 us -> 16.8 us
  between operations: 14.3 us -> 1.2 us
  local copies, waits for them, and re-layouts: 5.2 us -> 14.7 us
    reduce_scatter x1 -> x0, waiting for transfers between devices: 109 us -> none  [per_device(): lax.psum_scatter(partial_value.astype(jnp.float32).astype(jnp.bfloat16),...]
    all_gather x1 -> x0, waiting for transfers between devices: 64.9 us -> none  [per_device(): lax.all_gather(arrived.reshape(slot_count, arrived.shape[2]), 'mp', axis=...]
    all_to_all x1 -> x0, blocking collectives: 60.9 us -> none  [per_device(): lax.all_to_all(buffer[:-1].reshape((experts, capacity) + tokens.shape[1:]...]
    ppermute x0 -> x12, waiting for transfers between devices: none -> 45.1 us  [the longest x3 18.7 us: reduce_scatter_mp(): acc = acc + lax.ppermute(send, 'mp', shift_y(s)).astype(jnp.float32)]
    ppermute x0 -> x12, starting transfers between devices: none -> 43.1 us  [the longest x3 11.9 us: reduce_scatter_mp(): acc = acc + lax.ppermute(send, 'mp', shift_y(s)).astype(jnp.float32)]
    all_to_all x0 -> x1, waiting for transfers between devices: none -> 30.6 us  [per_device(): lax.all_to_all(buffer[:-1].reshape((experts, capacity) + tokens.shape[1:]...]
    all_to_all x0 -> x1, starting transfers between devices: none -> 30.4 us  [per_device(): lax.all_to_all(buffer[:-1].reshape((experts, capacity) + tokens.shape[1:]...]
    all_to_all x1, starting transfers between devices: 25.4 us -> 8.74 us  [per_device(): lax.all_to_all(summed.reshape(arrived.shape[0], capacity, summed.shape[1]...]
  transfers between devices with their start and end apart: 3 -> 14, of which waited for: 3 -> 12; matrix products, arithmetic and copies ran while one was open for 0% -> 1% of each run, Pallas kernels for 0% -> 0%
where the time goes in v1:
time: 230 us; the launch traced here: 227 us
  waiting for transfers between devices  106 us (46%)
  starting transfers between devices  82.2 us (36%)
  other arithmetic  16.8 us (7%)
  local copies, waits for them, and re-layouts  14.7 us (6%)
  matrix products  5.54 us (2%)
    all_to_all x1, waiting for transfers between devices, per_device(): lax.all_to_all(summed.reshape(arrived.shape[0], capacity, summed.shape[1]...  30.7 us
    all_to_all x1, waiting for transfers between devices, per_device(): lax.all_to_all(buffer[:-1].reshape((experts, capacity) + tokens.shape[1:]...  30.6 us
    all_to_all x1, starting transfers between devices, per_device(): lax.all_to_all(buffer[:-1].reshape((experts, capacity) + tokens.shape[1:]...  30.4 us
    ppermute x3, waiting for transfers between devices, reduce_scatter_mp(): acc = acc + lax.ppermute(send, 'mp', shift_y(s)).astype(jnp.float32)  18.7 us
    ppermute x3, waiting for transfers between devices, gather_mp(): lax.ppermute(along_x, 'mp', shift_y(s))  17.5 us
    ppermute x3, starting transfers between devices, reduce_scatter_mp(): acc = acc + lax.ppermute(send, 'mp', shift_y(s)).astype(jnp.float32)  11.9 us
    ppermute x3, starting transfers between devices, gather_mp(): lax.ppermute(along_x, 'mp', shift_y(s))  10.7 us
    ppermute x3, starting transfers between devices, gather_mp(): lax.ppermute(block, 'mp', shift_x(s))  10.5 us
  transfers between devices with their start and end apart: 14, of which 12 were waited for; matrix products, arithmetic and copies ran while one was open for 1% of the time, Pallas kernels for 0%

profile of v1, /device:TPU:1, one launch (start us, length us, event | category | flops | bytes accessed | tf_op | source)
XLA Modules:
  0.0 226.9 jit_solution(7285689925773911825)
XLA Ops:
  0.8 0.9 fusion.22
  1.7 0.2 reduce_window_sum.11
  1.9 0.8 select_reduce_fusion
  2.7 0.7 fusion.28
  3.4 1.3 scatter_custom_fusion
  4.8 0.7 reshape.231
  5.5 30.4 %all-to-all-start = ((bf16[64,4,256]{2,1,0:T(4,128)(2,1)}), bf16[64,4,256]{2,1,0:T(4,128)(2,1)S(1)}, u32[]{:S(2)}, u32[]{:S(2)}) async-start(bf16[64,4,256]{2,1,0:T(4,128)(2,1)} %reshape.231), calls=%async_computation | async-start | bytes 262144 | tf_op jit(solution)/shard_map/all_to_all | solution.py:90
  35.9 30.6 %all-to-all-done = bf16[64,4,256]{2,1,0:T(4,128)(2,1)S(1)} async-done(((bf16[64,4,256]{2,1,0:T(4,128)(2,1)}), bf16[64,4,256]{2,1,0:T(4,128)(2,1)S(1)}, u32[]{:S(2)}, u32[]{:S(2)}) %all-to-all-start) | async-done | bytes 131104 | tf_op jit(solution)/shard_map/all_to_all | solution.py:90
  66.6 3.1 %collective-permute-start = (bf16[256,256]{1,0:T(8,128)(2,1)S(1)}, bf16[256,256]{1,0:T(8,128)(2,1)}, u32[]{:S(2)}, u32[]{:S(2)}) collective-permute-start(bf16[256,256]{1,0:T(8,128)(2,1)S(1)} %reshape.232), channel_id=1, source_target_pairs={{0,1},{1,2},{2,3},{3,0},{4,5},{5,6},{6,7},{7,4},{8,9},{9,10},{10,1... | collective-permute-start | bytes 393224 | tf_op jit(solution)/shard_map/gather_along_x/ppermute | solution.py:40
  69.7 4.4 %collective-permute-start.1 = (bf16[256,256]{1,0:T(8,128)(2,1)S(1)}, bf16[256,256]{1,0:T(8,128)(2,1)}, u32[]{:S(2)}, u32[]{:S(2)}) collective-permute-start(bf16[256,256]{1,0:T(8,128)(2,1)S(1)} %reshape.232), channel_id=1, source_target_pairs={{0,2},{1,3},{2,0},{3,1},{4,6},{5,7},{6,4},{7,5},{8,10},{9,11},{10,... | collective-permute-start | bytes 393224 | tf_op jit(solution)/shard_map/gather_along_x/ppermute | solution.py:40
  74.1 3.1 %collective-permute-start.2 = (bf16[256,256]{1,0:T(8,128)(2,1)S(1)}, bf16[256,256]{1,0:T(8,128)(2,1)}, u32[]{:S(2)}, u32[]{:S(2)}) collective-permute-start(bf16[256,256]{1,0:T(8,128)(2,1)S(1)} %reshape.232), channel_id=1, source_target_pairs={{0,3},{1,0},{2,1},{3,2},{4,7},{5,4},{6,5},{7,6},{8,11},{9,8},{10,9... | collective-permute-start | bytes 393224 | tf_op jit(solution)/shard_map/gather_along_x/ppermute | solution.py:40
  77.2 0.0 collective-permute-done
  77.2 1.2 collective-permute-done.1
  78.4 1.5 collective-permute-done.2
  79.9 1.9 pad_maximum_fusion.1
  81.8 2.4 %gather_fusion = bf16[4,256,256]{2,1,0:T(8,128)(2,1)} fusion(bf16[4,256,256]{2,1,0:T(8,128)(2,1)} %pad_maximum_fusion.1, s32[1024]{0:T(1024)S(1)} %pad_clamp_fusion.2), kind=kCustom, calls=%fused_computation | custom fusion | bytes 1048592 | tf_op jit(solution)/shard_map/gather_along_x/jit(_take)/gather | solution.py:41
  84.2 2.0 broadcast_select_fusion.1
  86.2 3.2 %collective-permute-start.3 = (bf16[4,256,256]{2,1,0:T(8,128)(2,1)}, bf16[4,256,256]{2,1,0:T(8,128)(2,1)}, u32[]{:S(2)}, u32[]{:S(2)}) collective-permute-start(bf16[4,256,256]{2,1,0:T(8,128)(2,1)} %broadcast_select_fusion.1), channel_id=1, source_target_pairs={{0,4},{1,5},{2,6},{3,7},{4,8},{5,9},{6,10},{7,11},{8,12},{9,13},{1... | collective-permute-start | bytes 1572872 | tf_op jit(solution)/shard_map/gather_along_y/ppermute | solution.py:43
  89.4 4.5 %collective-permute-start.4 = (bf16[4,256,256]{2,1,0:T(8,128)(2,1)}, bf16[4,256,256]{2,1,0:T(8,128)(2,1)}, u32[]{:S(2)}, u32[]{:S(2)}) collective-permute-start(bf16[4,256,256]{2,1,0:T(8,128)(2,1)} %broadcast_select_fusion.1), channel_id=1, source_target_pairs={{0,8},{1,9},{2,10},{3,11},{4,12},{5,13},{6,14},{7,15},{8,0},{9,1},... | collective-permute-start | bytes 1572872 | tf_op jit(solution)/shard_map/gather_along_y/ppermute | solution.py:43
  93.9 3.0 %collective-permute-start.5 = (bf16[4,256,256]{2,1,0:T(8,128)(2,1)}, bf16[4,256,256]{2,1,0:T(8,128)(2,1)}, u32[]{:S(2)}, u32[]{:S(2)}) collective-permute-start(bf16[4,256,256]{2,1,0:T(8,128)(2,1)} %broadcast_select_fusion.1), channel_id=1, source_target_pairs={{0,12},{1,13},{2,14},{3,15},{4,0},{5,1},{6,2},{7,3},{8,4},{9,5},{1... | collective-permute-start | bytes 1572872 | tf_op jit(solution)/shard_map/gather_along_y/ppermute | solution.py:43
  97.0 1.2 bitcast_select_fusion
  98.1 1.7 collective-permute-done.3
  99.8 12.3 %collective-permute-done.4 = bf16[4,256,256]{2,1,0:T(8,128)(2,1)} collective-permute-done((bf16[4,256,256]{2,1,0:T(8,128)(2,1)}, bf16[4,256,256]{2,1,0:T(8,128)(2,1)}, u32[]{:S(2)}, u32[]{:S(2)}) %collective-permute-start.4) | collective-permute-done | bytes 524320 | tf_op jit(solution)/shard_map/gather_along_y/ppermute | solution.py:43
  112.1 3.6 %collective-permute-done.5 = bf16[4,256,256]{2,1,0:T(8,128)(2,1)} collective-permute-done((bf16[4,256,256]{2,1,0:T(8,128)(2,1)}, bf16[4,256,256]{2,1,0:T(8,128)(2,1)}, u32[]{:S(2)}, u32[]{:S(2)}) %collective-permute-start.5) | collective-permute-done | bytes 524320 | tf_op jit(solution)/shard_map/gather_along_y/ppermute | solution.py:43
  115.7 3.0 %pad_maximum_fusion = bf16[4,4,256,256]{3,2,1,0:T(8,128)(2,1)} fusion(bf16[1,4,256,256]{3,2,1,0:T(8,128)(2,1)} %bitcast.12, bf16[1,4,256,256]{3,2,1,0:T(8,128)(2,1)} %bitcast.11, bf16[1,4,256,256]{3,2,1,0:T(8,128)(2,1)} %bitcast.10, bf16[1,4,256,256]{3,2,1,0:T(8,128)(2,1)S(1)} %bitcast_select_fusion), kind=kLoop, calls=%fused_computation.4 | loop fusion | flops 3145728 | bytes 4194304 | tf_op jit(solution)/shard_map/gather_along_y/stack | solution.py:44
  118.6 3.6 %gather_fusion.1 = bf16[4,4,256,256]{3,2,1,0:T(8,128)(2,1)} fusion(bf16[4,4,256,256]{3,2,1,0:T(8,128)(2,1)} %pad_maximum_fusion, s32[1024]{0:T(1024)S(1)} %pad_clamp_fusion.1), kind=kCustom, calls=%fused_computation.1 | custom fusion | bytes 4194320 | tf_op jit(solution)/shard_map/gather_along_y/jit(_take)/gather | solution.py:44
  122.2 3.2 %broadcast_select_fusion = bf16[4,4,256,256]{3,2,1,0:T(8,128)(2,1)} fusion(bf16[4,4,256,256]{3,2,1,0:T(8,128)(2,1)} %gather_fusion.1, pred[4]{0:T(512)(128)(4,1)S(1)} %get-tuple-element.12), kind=kLoop, calls=%fused_computation.5 | loop fusion | flops 1048576 | bytes 4194308 | tf_op jit(solution)/shard_map/gather_along_y/jit(_take)/select_n | solution.py:44
  125.5 5.5 %convolution_convert_fusion = bf16[256,16,256]{2,0,1:T(8,128)(2,1)} fusion(bf16[16,256,384]{2,1,0:T(8,128)(2,1)S(1)} %bitcast.73, bf16[16,256,256]{2,1,0:T(8,128)(2,1)} %bitcast.76, bf16[1,256,384]{2,1,0:T(8,128)(2,1)S(1)} %copy-done.2), kind=kOutput, calls=%fused_computation.6 | convolution fusion | flops 1613627392 | bytes 7536640 | tf_op jit(solution)/shard_map/sf,jkf->jsk/dot_general | solution.py:108
  131.0 2.5 %dynamic-slice_bitcast_fusion.2 = (bf16[4,256,256]{2,1,0:T(8,128)(2,1)}, bf16[4,256,256]{2,1,0:T(8,128)(2,1)}, bf16[4,256,256]{2,1,0:T(8,128)(2,1)}) fusion(bf16[4,4,256,256]{3,2,1,0:T(8,128)(2,1)} %bitcast.74, s32[]{:T(128)S(6)} %select_n.241, s32[]{:T(128)S(6)} %select_n.245, s32[]{:T(128)S(6)} %select_n.243), kind=kLoop, calls=%fused_computation.17 | loop fusion | bytes 3145740 | tf_op jit(solution)/shard_map/reduce_along_y/jit(dynamic_index_in_dim)/squeeze | solution.py:56
  133.5 5.7 %collective-permute-start.6 = (bf16[4,256,256]{2,1,0:T(8,128)(2,1)}, bf16[4,256,256]{2,1,0:T(8,128)(2,1)}, u32[]{:S(2)}, u32[]{:S(2)}) collective-permute-start(bf16[4,256,256]{2,1,0:T(8,128)(2,1)} %get-tuple-element.5), channel_id=1, source_target_pairs={{0,4},{1,5},{2,6},{3,7},{4,8},{5,9},{6,10},{7,11},{8,12},{9,13},{1... | collective-permute-start | bytes 1572872 | tf_op jit(solution)/shard_map/reduce_along_y/ppermute | solution.py:57
  139.2 2.7 %collective-permute-start.7 = (bf16[4,256,256]{2,1,0:T(8,128)(2,1)}, bf16[4,256,256]{2,1,0:T(8,128)(2,1)}, u32[]{:S(2)}, u32[]{:S(2)}) collective-permute-start(bf16[4,256,256]{2,1,0:T(8,128)(2,1)} %get-tuple-element.7), channel_id=1, source_target_pairs={{0,8},{1,9},{2,10},{3,11},{4,12},{5,13},{6,14},{7,15},{8,0},{9,1},... | collective-permute-start | bytes 1572872 | tf_op jit(solution)/shard_map/reduce_along_y/ppermute | solution.py:57
  142.0 3.5 %collective-permute-start.8 = (bf16[4,256,256]{2,1,0:T(8,128)(2,1)}, bf16[4,256,256]{2,1,0:T(8,128)(2,1)}, u32[]{:S(2)}, u32[]{:S(2)}) collective-permute-start(bf16[4,256,256]{2,1,0:T(8,128)(2,1)} %get-tuple-element.6), channel_id=1, source_target_pairs={{0,12},{1,13},{2,14},{3,15},{4,0},{5,1},{6,2},{7,3},{8,4},{9,5},{1... | collective-permute-start | bytes 1572872 | tf_op jit(solution)/shard_map/reduce_along_y/ppermute | solution.py:57
  145.5 4.8 %collective-permute-done.6 = bf16[4,256,256]{2,1,0:T(8,128)(2,1)} collective-permute-done((bf16[4,256,256]{2,1,0:T(8,128)(2,1)}, bf16[4,256,256]{2,1,0:T(8,128)(2,1)}, u32[]{:S(2)}, u32[]{:S(2)}) %collective-permute-start.6) | collective-permute-done | bytes 524320 | tf_op jit(solution)/shard_map/reduce_along_y/ppermute | solution.py:57
  150.3 12.2 %collective-permute-done.7 = bf16[4,256,256]{2,1,0:T(8,128)(2,1)} collective-permute-done((bf16[4,256,256]{2,1,0:T(8,128)(2,1)}, bf16[4,256,256]{2,1,0:T(8,128)(2,1)}, u32[]{:S(2)}, u32[]{:S(2)}) %collective-permute-start.7) | collective-permute-done | bytes 524320 | tf_op jit(solution)/shard_map/reduce_along_y/ppermute | solution.py:57
  162.5 1.7 collective-permute-done.8
  164.3 1.8 fusion.1
  166.0 1.0 copy-done.1
  167.0 0.8 dynamic-slice_bitcast_fusion.5
  167.8 4.6 %collective-permute-start.10 = (f32[256,256]{1,0:T(8,128)}, f32[256,256]{1,0:T(8,128)}, u32[]{:S(2)}, u32[]{:S(2)}) collective-permute-start(f32[256,256]{1,0:T(8,128)} %get-tuple-element.10), channel_id=1, source_target_pairs={{0,2},{1,3},{2,0},{3,1},{4,6},{5,7},{6,4},{7,5},{8,10},{9,11},{10,... | collective-permute-start | bytes 786440 | tf_op jit(solution)/shard_map/reduce_along_x/ppermute | solution.py:62
  172.5 2.6 %collective-permute-start.11 = (f32[256,256]{1,0:T(8,128)}, f32[256,256]{1,0:T(8,128)}, u32[]{:S(2)}, u32[]{:S(2)}) collective-permute-start(f32[256,256]{1,0:T(8,128)} %get-tuple-element.9), channel_id=1, source_target_pairs={{0,3},{1,0},{2,1},{3,2},{4,7},{5,4},{6,5},{7,6},{8,11},{9,8},{10,9... | collective-permute-start | bytes 786440 | tf_op jit(solution)/shard_map/reduce_along_x/ppermute | solution.py:62
  175.1 2.7 %collective-permute-start.9 = (f32[256,256]{1,0:T(8,128)S(1)}, f32[256,256]{1,0:T(8,128)}, u32[]{:S(2)}, u32[]{:S(2)}) collective-permute-start(f32[256,256]{1,0:T(8,128)S(1)} %get-tuple-element.8), channel_id=1, source_target_pairs={{0,1},{1,2},{2,3},{3,0},{4,5},{5,6},{6,7},{7,4},{8,9},{9,10},{10,1... | collective-permute-start | bytes 786440 | tf_op jit(solution)/shard_map/reduce_along_x/ppermute | solution.py:62
  177.8 5.9 %collective-permute-done.11 = f32[256,256]{1,0:T(8,128)} collective-permute-done((f32[256,256]{1,0:T(8,128)}, f32[256,256]{1,0:T(8,128)}, u32[]{:S(2)}, u32[]{:S(2)}) %collective-permute-start.11) | collective-permute-done | bytes 262176 | tf_op jit(solution)/shard_map/reduce_along_x/ppermute | solution.py:62
  183.7 0.3 collective-permute-done.9
  184.0 1.2 fusion.12
  185.2 0.7 reshape.234
  185.9 8.7 %all-to-all-start.1 = ((bf16[64,4,256]{2,1,0:T(4,128)(2,1)}), bf16[64,4,256]{2,1,0:T(4,128)(2,1)S(1)}, u32[]{:S(2)}, u32[]{:S(2)}) async-start(bf16[64,4,256]{2,1,0:T(4,128)(2,1)} %reshape.234), calls=%async_computation.1 | async-start | bytes 262144 | tf_op jit(solution)/shard_map/all_to_all | solution.py:112
  194.7 30.7 %all-to-all-done.1 = bf16[64,4,256]{2,1,0:T(4,128)(2,1)S(1)} async-done(((bf16[64,4,256]{2,1,0:T(4,128)(2,1)}), bf16[64,4,256]{2,1,0:T(4,128)(2,1)S(1)}, u32[]{:S(2)}, u32[]{:S(2)}) %all-to-all-start.1) | async-done | bytes 131104 | tf_op jit(solution)/shard_map/all_to_all | solution.py:112
  225.4 1.5 gather_fusion.2
  (18 shorter events, 0.2 us)
Async XLA Ops:
  0.0 125.4 %copy-start = (bf16[1,4096,384]{2,1,0:T(8,128)(2,1)S(1)}, bf16[1,4096,384]{2,1,0:T(8,128)(2,1)}, u32[]{:S(2)}) copy-start(bf16[1,4096,384]{2,1,0:T(8,128)(2,1)} %param.9) | copy-start | bytes 9437188
  5.5 61.1 %all-to-all-start = ((bf16[64,4,256]{2,1,0:T(4,128)(2,1)}), bf16[64,4,256]{2,1,0:T(4,128)(2,1)S(1)}, u32[]{:S(2)}, u32[]{:S(2)}) async-start(bf16[64,4,256]{2,1,0:T(4,128)(2,1)} %reshape.231), calls=%async_computation | async-start | bytes 262144 | tf_op jit(solution)/shard_map/all_to_all | solution.py:90
  66.6 10.6 %collective-permute-start = (bf16[256,256]{1,0:T(8,128)(2,1)S(1)}, bf16[256,256]{1,0:T(8,128)(2,1)}, u32[]{:S(2)}, u32[]{:S(2)}) collective-permute-start(bf16[256,256]{1,0:T(8,128)(2,1)S(1)} %reshape.232), channel_id=1, source_target_pairs={{0,1},{1,2},{2,3},{3,0},{4,5},{5,6},{6,7},{7,4},{8,9},{9,10},{10,1... | collective-permute-start | bytes 393224 | tf_op jit(solution)/shard_map/gather_along_x/ppermute | solution.py:40
  69.7 8.7 %collective-permute-start.1 = (bf16[256,256]{1,0:T(8,128)(2,1)S(1)}, bf16[256,256]{1,0:T(8,128)(2,1)}, u32[]{:S(2)}, u32[]{:S(2)}) collective-permute-start(bf16[256,256]{1,0:T(8,128)(2,1)S(1)} %reshape.232), channel_id=1, source_target_pairs={{0,2},{1,3},{2,0},{3,1},{4,6},{5,7},{6,4},{7,5},{8,10},{9,11},{10,... | collective-permute-start | bytes 393224 | tf_op jit(solution)/shard_map/gather_along_x/ppermute | solution.py:40
  74.1 5.8 %collective-permute-start.2 = (bf16[256,256]{1,0:T(8,128)(2,1)S(1)}, bf16[256,256]{1,0:T(8,128)(2,1)}, u32[]{:S(2)}, u32[]{:S(2)}) collective-permute-start(bf16[256,256]{1,0:T(8,128)(2,1)S(1)} %reshape.232), channel_id=1, source_target_pairs={{0,3},{1,0},{2,1},{3,2},{4,7},{5,4},{6,5},{7,6},{8,11},{9,8},{10,9... | collective-permute-start | bytes 393224 | tf_op jit(solution)/shard_map/gather_along_x/ppermute | solution.py:40
  86.2 13.6 %collective-permute-start.3 = (bf16[4,256,256]{2,1,0:T(8,128)(2,1)}, bf16[4,256,256]{2,1,0:T(8,128)(2,1)}, u32[]{:S(2)}, u32[]{:S(2)}) collective-permute-start(bf16[4,256,256]{2,1,0:T(8,128)(2,1)} %broadcast_select_fusion.1), channel_id=1, source_target_pairs={{0,4},{1,5},{2,6},{3,7},{4,8},{5,9},{6,10},{7,11},{8,12},{9,13},{1... | collective-permute-start | bytes 1572872 | tf_op jit(solution)/shard_map/gather_along_y/ppermute | solution.py:43
  89.4 22.8 %collective-permute-start.4 = (bf16[4,256,256]{2,1,0:T(8,128)(2,1)}, bf16[4,256,256]{2,1,0:T(8,128)(2,1)}, u32[]{:S(2)}, u32[]{:S(2)}) collective-permute-start(bf16[4,256,256]{2,1,0:T(8,128)(2,1)} %broadcast_select_fusion.1), channel_id=1, source_target_pairs={{0,8},{1,9},{2,10},{3,11},{4,12},{5,13},{6,14},{7,15},{8,0},{9,1},... | collective-permute-start | bytes 1572872 | tf_op jit(solution)/shard_map/gather_along_y/ppermute | solution.py:43
  93.9 21.8 %collective-permute-start.5 = (bf16[4,256,256]{2,1,0:T(8,128)(2,1)}, bf16[4,256,256]{2,1,0:T(8,128)(2,1)}, u32[]{:S(2)}, u32[]{:S(2)}) collective-permute-start(bf16[4,256,256]{2,1,0:T(8,128)(2,1)} %broadcast_select_fusion.1), channel_id=1, source_target_pairs={{0,12},{1,13},{2,14},{3,15},{4,0},{5,1},{6,2},{7,3},{8,4},{9,5},{1... | collective-permute-start | bytes 1572872 | tf_op jit(solution)/shard_map/gather_along_y/ppermute | solution.py:43
  122.2 3.2 %copy-start.2 = (bf16[1,256,384]{2,1,0:T(8,128)(2,1)S(1)}, bf16[1,256,384]{2,1,0:T(8,128)(2,1)}, u32[]{:S(2)}) copy-start(bf16[1,256,384]{2,1,0:T(8,128)(2,1)} %param.8) | copy-start | bytes 589828
  133.5 16.8 %collective-permute-start.6 = (bf16[4,256,256]{2,1,0:T(8,128)(2,1)}, bf16[4,256,256]{2,1,0:T(8,128)(2,1)}, u32[]{:S(2)}, u32[]{:S(2)}) collective-permute-start(bf16[4,256,256]{2,1,0:T(8,128)(2,1)} %get-tuple-element.5), channel_id=1, source_target_pairs={{0,4},{1,5},{2,6},{3,7},{4,8},{5,9},{6,10},{7,11},{8,12},{9,13},{1... | collective-permute-start | bytes 1572872 | tf_op jit(solution)/shard_map/reduce_along_y/ppermute | solution.py:57
  139.2 23.3 %collective-permute-start.7 = (bf16[4,256,256]{2,1,0:T(8,128)(2,1)}, bf16[4,256,256]{2,1,0:T(8,128)(2,1)}, u32[]{:S(2)}, u32[]{:S(2)}) collective-permute-start(bf16[4,256,256]{2,1,0:T(8,128)(2,1)} %get-tuple-element.7), channel_id=1, source_target_pairs={{0,8},{1,9},{2,10},{3,11},{4,12},{5,13},{6,14},{7,15},{8,0},{9,1},... | collective-permute-start | bytes 1572872 | tf_op jit(solution)/shard_map/reduce_along_y/ppermute | solution.py:57
  142.0 22.3 %collective-permute-start.8 = (bf16[4,256,256]{2,1,0:T(8,128)(2,1)}, bf16[4,256,256]{2,1,0:T(8,128)(2,1)}, u32[]{:S(2)}, u32[]{:S(2)}) collective-permute-start(bf16[4,256,256]{2,1,0:T(8,128)(2,1)} %get-tuple-element.6), channel_id=1, source_target_pairs={{0,12},{1,13},{2,14},{3,15},{4,0},{5,1},{6,2},{7,3},{8,4},{9,5},{1... | collective-permute-start | bytes 1572872 | tf_op jit(solution)/shard_map/reduce_along_y/ppermute | solution.py:57
  166.0 1.0 copy-start.1
  167.8 10.0 %collective-permute-start.10 = (f32[256,256]{1,0:T(8,128)}, f32[256,256]{1,0:T(8,128)}, u32[]{:S(2)}, u32[]{:S(2)}) collective-permute-start(f32[256,256]{1,0:T(8,128)} %get-tuple-element.10), channel_id=1, source_target_pairs={{0,2},{1,3},{2,0},{3,1},{4,6},{5,7},{6,4},{7,5},{8,10},{9,11},{10,... | collective-permute-start | bytes 786440 | tf_op jit(solution)/shard_map/reduce_along_x/ppermute | solution.py:62
  172.5 11.2 %collective-permute-start.11 = (f32[256,256]{1,0:T(8,128)}, f32[256,256]{1,0:T(8,128)}, u32[]{:S(2)}, u32[]{:S(2)}) collective-permute-start(f32[256,256]{1,0:T(8,128)} %get-tuple-element.9), channel_id=1, source_target_pairs={{0,3},{1,0},{2,1},{3,2},{4,7},{5,4},{6,5},{7,6},{8,11},{9,8},{10,9... | collective-permute-start | bytes 786440 | tf_op jit(solution)/shard_map/reduce_along_x/ppermute | solution.py:62
  175.1 8.9 %collective-permute-start.9 = (f32[256,256]{1,0:T(8,128)S(1)}, f32[256,256]{1,0:T(8,128)}, u32[]{:S(2)}, u32[]{:S(2)}) collective-permute-start(f32[256,256]{1,0:T(8,128)S(1)} %get-tuple-element.8), channel_id=1, source_target_pairs={{0,1},{1,2},{2,3},{3,0},{4,5},{5,6},{6,7},{7,4},{8,9},{9,10},{10,1... | collective-permute-start | bytes 786440 | tf_op jit(solution)/shard_map/reduce_along_x/ppermute | solution.py:62
  185.9 39.4 %all-to-all-start.1 = ((bf16[64,4,256]{2,1,0:T(4,128)(2,1)}), bf16[64,4,256]{2,1,0:T(4,128)(2,1)S(1)}, u32[]{:S(2)}, u32[]{:S(2)}) async-start(bf16[64,4,256]{2,1,0:T(4,128)(2,1)} %reshape.234), calls=%async_computation.1 | async-start | bytes 262144 | tf_op jit(solution)/shard_map/all_to_all | solution.py:112

commit v2 on v0

--- a/solution.py
+++ b/solution.py
@@ -14,6 +14,17 @@
     return 0.5 * (1.0 + squashed) + 0.5 * preact * (1.0 - squashed * squashed) * coeff * (
         1.0 + 3.0 * 0.044715 * preact * preact
     )
+
+
+def gather_mp(block):
+    n_mp = lax.axis_size("mp")
+    copies = jnp.broadcast_to(block[None], (n_mp,) + block.shape)
+    return lax.all_to_all(copies, "mp", split_axis=0, concat_axis=0, tiled=True)
+
+
+def reduce_scatter_mp(parts):
+    arrived = lax.all_to_all(parts, "mp", split_axis=0, concat_axis=0, tiled=True)
+    return jnp.sum(arrived.astype(jnp.float32), axis=0)
 
 
 def per_device(tokens, expert_ids, seq_lengths, hidden_cotangent, w_in):
@@ -48,24 +59,20 @@
         tiled=True,
     )
     slot_count = arrived.shape[0] * capacity
-    features = lax.all_gather(
-        arrived.reshape(slot_count, arrived.shape[2]), "mp", axis=1, tiled=True
+    n_mp = lax.axis_size("mp")
+    blocks = gather_mp(arrived.reshape(slot_count, arrived.shape[2]))
+    weight = w_in[0]
+    weight_blocks = weight.reshape((n_mp, weight.shape[0] // n_mp, weight.shape[1]))
+    pre_act = jnp.einsum(
+        "jsk,jkf->sf", blocks, weight_blocks, preferred_element_type=jnp.float32
     )
-    weight = w_in[0]
-    pre_act = jnp.dot(features, weight, preferred_element_type=jnp.float32)
     hidden_grad = (hidden_cotangent[0].astype(jnp.float32) * gelu_slope(pre_act)).astype(
         jnp.bfloat16
     )
-    partial_value = lax.dot_general(
-        hidden_grad, weight, (((1,), (1,)), ((), ())), preferred_element_type=jnp.float32
+    block_parts = jnp.einsum(
+        "sf,jkf->jsk", hidden_grad, weight_blocks, preferred_element_type=jnp.float32
     ).astype(jnp.bfloat16)
-    partial_value = lax.optimization_barrier(partial_value)
-    summed = lax.psum_scatter(
-        partial_value.astype(jnp.float32).astype(jnp.bfloat16),
-        "mp",
-        scatter_dimension=1,
-        tiled=True,
-    )
+    summed = reduce_scatter_mp(block_parts).astype(jnp.bfloat16)
     returned = lax.all_to_all(
         summed.reshape(arrived.shape[0], capacity, summed.shape[1]),
         "expert",

time: 319 us -> 179 us (0.56)
  waiting for transfers between devices: 205 us -> 30.7 us
  blocking collectives: 60.9 us -> 124 us
  starting transfers between devices: 25.5 us -> 9.25 us
  between operations: 14.3 us -> 0.89 us
    reduce_scatter x1 -> x0, waiting for transfers between devices: 109 us -> none  [per_device(): lax.psum_scatter(partial_value.astype(jnp.float32).astype(jnp.bfloat16),...]
    all_gather x1 -> x0, waiting for transfers between devices: 64.9 us -> none  [per_device(): lax.all_gather(arrived.reshape(slot_count, arrived.shape[2]), 'mp', axis=...]
    all_to_all x0 -> x2, blocking collectives: none -> 63.4 us  [the longest x1 33.5 us: gather_mp(): return lax.all_to_all(copies, 'mp', split_axis=0, concat_axis=0, tiled=True)]
    all_to_all x1, starting transfers between devices: 25.4 us -> 9.25 us  [per_device(): lax.all_to_all(summed.reshape(arrived.shape[0], capacity, summed.shape[1]...]
  transfers between devices with their start and end apart: 3 -> 1, of which waited for: 3 -> 1; matrix products, arithmetic and copies ran while one was open for 0% -> 0% of each run, Pallas kernels for 0% -> 0%
where the time goes in v2:
time: 179 us
  blocking collectives  124 us (69%)
  waiting for transfers between devices  30.7 us (17%)
  starting transfers between devices  9.25 us (5%)
  matrix products  5.56 us (3%)
  other arithmetic  4.46 us (2%)
  local copies, waits for them, and re-layouts  3.83 us (2%)
    all_to_all x1, blocking collectives, per_device(): lax.all_to_all(buffer[:-1].reshape((experts, capacity) + tokens.shape[1:]...  60.9 us
    all_to_all x1, blocking collectives, gather_mp(): return lax.all_to_all(copies, 'mp', split_axis=0, concat_axis=0, tiled=True)  33.5 us
    all_to_all x1, waiting for transfers between devices, per_device(): lax.all_to_all(summed.reshape(arrived.shape[0], capacity, summed.shape[1]...  30.7 us
    all_to_all x1, blocking collectives, reduce_scatter_mp(): lax.all_to_all(parts, 'mp', split_axis=0, concat_axis=0, tiled=True)  29.9 us
    all_to_all x1, starting transfers between devices, per_device(): lax.all_to_all(summed.reshape(arrived.shape[0], capacity, summed.shape[1]...  9.25 us
    dot_general x1, matrix products, per_device(): jnp.einsum('sf,jkf->jsk', hidden_grad, weight_blocks, preferred_element_t...  5.56 us
  transfers between devices with their start and end apart: 1, of which 1 were waited for; matrix products, arithmetic and copies ran while one was open for 0% of the time, Pallas kernels for 0%

profile of v2, /device:TPU:1, one launch (start us, length us, event | category | flops | bytes accessed | tf_op | source)
XLA Modules:
  0.0 178.9 jit_solution(10910733681043657541)
XLA Ops:
  0.0 0.0 copy-start
  0.8 0.9 fusion.17
  1.7 0.2 reduce_window_sum.11
  1.9 0.8 select_reduce_fusion
  2.7 0.7 fusion.19
  3.4 1.3 scatter_custom_fusion
  4.8 60.9 %all_to_all.20 = bf16[64,4,256]{2,1,0:T(4,128)(2,1)S(1)} all-to-all(bf16[64,4,256]{2,1,0:T(4,128)(2,1)S(1)} %reshape.88), channel_id=1, replica_groups=mesh['expert'=64,'mp'=16] {'expert'}, dimensions={0} | all-to-all | bytes 262144 | tf_op jit(solution)/shard_map/all_to_all | solution.py:54
  65.7 0.2 broadcast_in_dim.41
  65.9 0.0 copy-start.1
  65.9 33.5 %all_to_all.21 = bf16[16,256,256]{2,1,0:T(8,128)(2,1)} all-to-all(bf16[16,256,256]{2,1,0:T(8,128)(2,1)S(1)} %broadcast_in_dim.41), channel_id=1, replica_groups=mesh['expert'=64,'mp'=16] {'mp'}, dimensions={0} | all-to-all | bytes 4194304 | tf_op jit(solution)/shard_map/all_to_all | solution.py:22
  99.4 0.0 copy-done
  99.4 0.0 copy-done.1
  99.4 5.6 %convert_bitcast_fusion = bf16[16,256,256]{2,1,0:T(8,128)(2,1)} fusion(bf16[16,256,384]{2,1,0:T(8,128)(2,1)S(1)} %bitcast.36, bf16[16,256,256]{2,1,0:T(8,128)(2,1)} %all_to_all.21, bf16[1,256,384]{2,1,0:T(8,128)(2,1)S(1)} %copy-done.1), kind=kOutput, calls=%fused_computation.2 | convolution fusion | flops 1613627392 | bytes 7536640 | tf_op jit(solution)/shard_map/sf,jkf->jsk/dot_general | solution.py:72
  105.0 29.9 %all_to_all.22 = bf16[16,256,256]{2,1,0:T(8,128)(2,1)} all-to-all(bf16[16,256,256]{2,1,0:T(8,128)(2,1)} %convert_bitcast_fusion), channel_id=1, replica_groups=mesh['expert'=64,'mp'=16] {'mp'}, dimensions={0} | all-to-all | bytes 4194304 | tf_op jit(solution)/shard_map/all_to_all | solution.py:26
  134.9 1.9 %reduce_sum.26 = bf16[256,256]{1,0:T(8,128)(2,1)S(1)} reduce(bf16[16,256,256]{2,1,0:T(8,128)(2,1)} %all_to_all.22, bf16[]{:T(256)} %constant.48.clone.1), dimensions={0}, to_apply=%region_3.4 | reduce | flops 983040 | bytes 2228226 | tf_op jit(solution)/shard_map/reduce_sum | solution.py:27
  136.8 0.7 reshape.89
  137.5 9.2 %all-to-all-start.3 = ((bf16[64,4,256]{2,1,0:T(4,128)(2,1)}), bf16[64,4,256]{2,1,0:T(4,128)(2,1)S(1)}, u32[]{:S(2)}, u32[]{:S(2)}) async-start(bf16[64,4,256]{2,1,0:T(4,128)(2,1)} %reshape.89), calls=%async_computation.3 | async-start | bytes 262144 | tf_op jit(solution)/shard_map/all_to_all | solution.py:76
  146.7 30.7 %all-to-all-done.3 = bf16[64,4,256]{2,1,0:T(4,128)(2,1)S(1)} async-done(((bf16[64,4,256]{2,1,0:T(4,128)(2,1)}), bf16[64,4,256]{2,1,0:T(4,128)(2,1)S(1)}, u32[]{:S(2)}, u32[]{:S(2)}) %all-to-all-start.3) | async-done | bytes 131104 | tf_op jit(solution)/shard_map/all_to_all | solution.py:76
  177.5 1.5 gather_fusion
  (7 shorter events, 0.1 us)
Async XLA Ops:
  0.0 99.4 %copy-start = (bf16[1,4096,384]{2,1,0:T(8,128)(2,1)S(1)}, bf16[1,4096,384]{2,1,0:T(8,128)(2,1)}, u32[]{:S(2)}) copy-start(bf16[1,4096,384]{2,1,0:T(8,128)(2,1)} %param.9) | copy-start | bytes 9437188
  65.9 33.5 %copy-start.1 = (bf16[1,256,384]{2,1,0:T(8,128)(2,1)S(1)}, bf16[1,256,384]{2,1,0:T(8,128)(2,1)}, u32[]{:S(2)}) copy-start(bf16[1,256,384]{2,1,0:T(8,128)(2,1)} %param.8) | copy-start | bytes 589828
  137.5 39.9 %all-to-all-start.3 = ((bf16[64,4,256]{2,1,0:T(4,128)(2,1)}), bf16[64,4,256]{2,1,0:T(4,128)(2,1)S(1)}, u32[]{:S(2)}, u32[]{:S(2)}) async-start(bf16[64,4,256]{2,1,0:T(4,128)(2,1)} %reshape.89), calls=%async_computation.3 | async-start | bytes 262144 | tf_op jit(solution)/shard_map/all_to_all | solution.py:76

commit v3 on v2

--- a/solution.py
+++ b/solution.py
@@ -3,7 +3,7 @@
 import jax
 import jax.numpy as jnp
 from jax import lax
-from jax.sharding import PartitionSpec as P
+from jax.sharding import Mesh, PartitionSpec as P
 
 SEQ_LEN = 128
 
@@ -27,9 +27,22 @@
     return jnp.sum(arrived.astype(jnp.float32), axis=0)
 
 
+def exchange_experts(rows, back):
+    n_ez, n_core = lax.axis_size("ez"), lax.axis_size("core")
+    grid = rows.reshape((n_ez, n_core) + rows.shape[1:])
+    if back:
+        grid = lax.all_to_all(grid, "ez", split_axis=0, concat_axis=0, tiled=True)
+        grid = lax.all_to_all(grid, "core", split_axis=1, concat_axis=1, tiled=True)
+    else:
+        grid = lax.all_to_all(grid, "core", split_axis=1, concat_axis=1, tiled=True)
+        grid = lax.all_to_all(grid, "ez", split_axis=0, concat_axis=0, tiled=True)
+    return grid.reshape(rows.shape)
+
+
 def per_device(tokens, expert_ids, seq_lengths, hidden_cotangent, w_in):
     tok_dev = tokens.shape[0]
-    experts = w_in.shape[0] * lax.axis_size("expert")
+    n_ez, n_core = lax.axis_size("ez"), lax.axis_size("core")
+    experts = w_in.shape[0] * n_ez * n_core
     capacity = max(2, 2 * tok_dev // experts)
     position = jnp.arange(tok_dev, dtype=jnp.int32)
     seq_index = position // SEQ_LEN
@@ -51,13 +64,7 @@
     buffer = (
         jnp.zeros((experts * capacity + 1,) + tokens.shape[1:], tokens.dtype).at[target].set(tokens)
     )
-    arrived = lax.all_to_all(
-        buffer[:-1].reshape((experts, capacity) + tokens.shape[1:]),
-        "expert",
-        split_axis=0,
-        concat_axis=0,
-        tiled=True,
-    )
+    arrived = exchange_experts(buffer[:-1].reshape((experts, capacity) + tokens.shape[1:]), False)
     slot_count = arrived.shape[0] * capacity
     n_mp = lax.axis_size("mp")
     blocks = gather_mp(arrived.reshape(slot_count, arrived.shape[2]))
@@ -73,13 +80,7 @@
         "sf,jkf->jsk", hidden_grad, weight_blocks, preferred_element_type=jnp.float32
     ).astype(jnp.bfloat16)
     summed = reduce_scatter_mp(block_parts).astype(jnp.bfloat16)
-    returned = lax.all_to_all(
-        summed.reshape(arrived.shape[0], capacity, summed.shape[1]),
-        "expert",
-        split_axis=0,
-        concat_axis=0,
-        tiled=True,
-    )
+    returned = exchange_experts(summed.reshape(arrived.shape[0], capacity, summed.shape[1]), True)
     flat_rows = returned.reshape((experts * capacity,) + returned.shape[2:])
     padded = jnp.concatenate(
         [flat_rows, jnp.zeros((1,) + flat_rows.shape[1:], flat_rows.dtype)], axis=0
@@ -88,14 +89,18 @@
 
 
 def solution(mesh):
+    n_expert, n_mp = mesh.shape["expert"], mesh.shape["mp"]
+    cores = 2
+    split = Mesh(mesh.devices.reshape(n_expert // cores, cores, n_mp), ("ez", "core", "mp"))
+    expert = ("ez", "core")
     in_specs = (
-        P("expert", "mp"),
-        P("expert", None),
-        P("expert"),
-        P("expert", None, "mp"),
-        P("expert", None, "mp"),
+        P(expert, "mp"),
+        P(expert, None),
+        P(expert),
+        P(expert, None, "mp"),
+        P(expert, None, "mp"),
     )
-    out_specs = P("expert", "mp")
+    out_specs = P(expert, "mp")
     return jax.shard_map(
-        per_device, mesh=mesh, in_specs=in_specs, out_specs=out_specs, check_vma=False
+        per_device, mesh=split, in_specs=in_specs, out_specs=out_specs, check_vma=False
     )

time: 179 us -> 184 us (1.028)
  blocking collectives: 124 us -> 134 us
  waiting for transfers between devices: 30.7 us -> 26.4 us
    all_to_all x1 -> x3, blocking collectives: 60.9 us -> 72.6 us  [the longest x1 45.4 us: exchange_experts(): grid = lax.all_to_all(grid, 'ez', split_axis=0, concat_axis=0, tiled=True)]
    all_to_all x1, waiting for transfers between devices: 30.7 us -> 26.4 us  [exchange_experts(): grid = lax.all_to_all(grid, 'ez', split_axis=0, concat_axis=0, tiled=True)]
where the time goes in v3:
time: 184 us; the launch traced here: 183 us
  blocking collectives  134 us (73%)
  waiting for transfers between devices  26.4 us (14%)
  starting transfers between devices  8.05 us (4%)
  matrix products  5.55 us (3%)
  other arithmetic  4.46 us (2%)
  local copies, waits for them, and re-layouts  4.02 us (2%)
    all_to_all x1, blocking collectives, exchange_experts(): grid = lax.all_to_all(grid, 'ez', split_axis=0, concat_axis=0, tiled=True)  45.4 us
    all_to_all x1, blocking collectives, gather_mp(): return lax.all_to_all(copies, 'mp', split_axis=0, concat_axis=0, tiled=True)  32.2 us
    all_to_all x1, blocking collectives, reduce_scatter_mp(): lax.all_to_all(parts, 'mp', split_axis=0, concat_axis=0, tiled=True)  28.9 us
    all_to_all x2, blocking collectives, exchange_experts(): grid = lax.all_to_all(grid, 'core', split_axis=1, concat_axis=1, tiled=True)  27.1 us
    all_to_all x1, waiting for transfers between devices, exchange_experts(): grid = lax.all_to_all(grid, 'ez', split_axis=0, concat_axis=0, tiled=True)  26.4 us
    all_to_all x1, starting transfers between devices, exchange_experts(): grid = lax.all_to_all(grid, 'ez', split_axis=0, concat_axis=0, tiled=True)  8.05 us
    dot_general x1, matrix products, per_device(): jnp.einsum('sf,jkf->jsk', hidden_grad, weight_blocks, preferred_element_t...  5.55 us
  transfers between devices with their start and end apart: 1, of which 1 were waited for; matrix products, arithmetic and copies ran while one was open for 0% of the time, Pallas kernels for 0%

profile of v3, /device:TPU:1, one launch (start us, length us, event | category | flops | bytes accessed | tf_op | source)
XLA Modules:
  0.0 183.1 jit_solution(11366593872180142199)
XLA Ops:
  0.0 0.0 copy-start
  0.8 0.9 fusion.17
  1.7 0.2 reduce_window_sum.11
  1.9 0.8 select_reduce_fusion
  2.7 0.7 fusion.19
  3.4 1.3 scatter_custom_fusion
  4.9 17.6 %all_to_all.30 = bf16[32,2,4,256]{3,2,0,1:T(4,128)(2,1)S(1)} all-to-all(bf16[32,2,4,256]{3,2,0,1:T(4,128)(2,1)S(1)} %copy.12), channel_id=1, replica_groups=mesh['ez'=32,'core'=2,'mp'=16] {'core'}, dimensions={1} | all-to-all | bytes 262144 | tf_op jit(solution)/shard_map/all_to_all | solution.py:37
  22.6 45.4 %all_to_all.31 = bf16[32,2,4,256]{3,2,1,0:T(4,128)(2,1)S(1)} all-to-all(bf16[32,2,4,256]{3,2,1,0:T(4,128)(2,1)S(1)} %copy.13), channel_id=1, replica_groups=mesh['ez'=32,'core'=2,'mp'=16] {'ez'}, dimensions={0} | all-to-all | bytes 262144 | tf_op jit(solution)/shard_map/all_to_all | solution.py:38
  68.0 0.2 broadcast_in_dim.41
  68.2 0.0 copy-start.1
  68.2 32.2 %all_to_all.32 = bf16[16,256,256]{2,1,0:T(8,128)(2,1)} all-to-all(bf16[16,256,256]{2,1,0:T(8,128)(2,1)S(1)} %broadcast_in_dim.41), channel_id=1, replica_groups=mesh['ez'=32,'core'=2,'mp'=16] {'mp'}, dimensions={0} | all-to-all | bytes 4194304 | tf_op jit(solution)/shard_map/all_to_all | solution.py:22
  100.5 0.0 copy-done
  100.5 0.0 copy-done.1
  100.5 5.6 %convert_bitcast_fusion = bf16[16,256,256]{2,1,0:T(8,128)(2,1)} fusion(bf16[16,256,384]{2,1,0:T(8,128)(2,1)S(1)} %bitcast.36, bf16[16,256,256]{2,1,0:T(8,128)(2,1)} %all_to_all.32, bf16[1,256,384]{2,1,0:T(8,128)(2,1)S(1)} %copy-done.1), kind=kOutput, calls=%fused_computation.2 | convolution fusion | flops 1613627392 | bytes 7536640 | tf_op jit(solution)/shard_map/sf,jkf->jsk/dot_general | solution.py:79
  106.0 28.9 %all_to_all.33 = bf16[16,256,256]{2,1,0:T(8,128)(2,1)} all-to-all(bf16[16,256,256]{2,1,0:T(8,128)(2,1)} %convert_bitcast_fusion), channel_id=1, replica_groups=mesh['ez'=32,'core'=2,'mp'=16] {'mp'}, dimensions={0} | all-to-all | bytes 4194304 | tf_op jit(solution)/shard_map/all_to_all | solution.py:26
  134.9 1.9 %reduce_sum.26 = bf16[256,256]{1,0:T(8,128)(2,1)S(1)} reduce(bf16[16,256,256]{2,1,0:T(8,128)(2,1)} %all_to_all.33, bf16[]{:T(256)} %constant.48.clone.1), dimensions={0}, to_apply=%region_3.4 | reduce | flops 983040 | bytes 2228226 | tf_op jit(solution)/shard_map/reduce_sum | solution.py:27
  136.8 0.7 reshape_reshape.10
  137.5 8.1 %all-to-all-start.4 = ((bf16[32,2,4,256]{3,2,1,0:T(4,128)(2,1)}), bf16[32,2,4,256]{3,2,1,0:T(4,128)(2,1)S(1)}, u32[]{:S(2)}, u32[]{:S(2)}) async-start(bf16[32,2,4,256]{3,2,1,0:T(4,128)(2,1)} %reshape_reshape.10), calls=%async_computation.4 | async-start | bytes 262144 | tf_op jit(solution)/shard_map/all_to_all | solution.py:34
  145.6 26.4 %all-to-all-done.4 = bf16[32,2,4,256]{3,2,1,0:T(4,128)(2,1)S(1)} async-done(((bf16[32,2,4,256]{3,2,1,0:T(4,128)(2,1)}), bf16[32,2,4,256]{3,2,1,0:T(4,128)(2,1)S(1)}, u32[]{:S(2)}, u32[]{:S(2)}) %all-to-all-start.4) | async-done | bytes 131104 | tf_op jit(solution)/shard_map/all_to_all | solution.py:34
  172.0 9.5 %all_to_all.34 = bf16[32,2,4,256]{3,2,0,1:T(4,128)(2,1)S(1)} all-to-all(bf16[32,2,4,256]{3,2,0,1:T(4,128)(2,1)S(1)} %copy.14), channel_id=1, replica_groups=mesh['ez'=32,'core'=2,'mp'=16] {'core'}, dimensions={1} | all-to-all | bytes 262144 | tf_op jit(solution)/shard_map/all_to_all | solution.py:35
  181.6 1.5 gather_fusion
  (11 shorter events, 0.3 us)
Async XLA Ops:
  0.0 100.5 %copy-start = (bf16[1,4096,384]{2,1,0:T(8,128)(2,1)S(1)}, bf16[1,4096,384]{2,1,0:T(8,128)(2,1)}, u32[]{:S(2)}) copy-start(bf16[1,4096,384]{2,1,0:T(8,128)(2,1)} %param.9) | copy-start | bytes 9437188
  68.2 32.2 %copy-start.1 = (bf16[1,256,384]{2,1,0:T(8,128)(2,1)S(1)}, bf16[1,256,384]{2,1,0:T(8,128)(2,1)}, u32[]{:S(2)}) copy-start(bf16[1,256,384]{2,1,0:T(8,128)(2,1)} %param.8) | copy-start | bytes 589828
  137.5 34.4 %all-to-all-start.4 = ((bf16[32,2,4,256]{3,2,1,0:T(4,128)(2,1)}), bf16[32,2,4,256]{3,2,1,0:T(4,128)(2,1)S(1)}, u32[]{:S(2)}, u32[]{:S(2)}) async-start(bf16[32,2,4,256]{3,2,1,0:T(4,128)(2,1)} %reshape_reshape.10), calls=%async_computation.4 | async-start | bytes 262144 | tf_op jit(solution)/shard_map/all_to_all | solution.py:34

commit v4 on v2

--- a/solution.py
+++ b/solution.py
@@ -43,16 +43,19 @@
     )
     live_mask = position % SEQ_LEN < seq_length
     expert_row = expert_ids[:, 0]
-    onehot = (
-        (expert_row[:, None] == jnp.arange(experts, dtype=jnp.int32)[None, :]) & live_mask[:, None]
-    ).astype(jnp.int32)
-    slot_rank = jnp.sum(jnp.cumsum(onehot, axis=0) * onehot, axis=1) - 1
-    target = jnp.where(live_mask, expert_row * capacity + slot_rank, experts * capacity)
-    buffer = (
-        jnp.zeros((experts * capacity + 1,) + tokens.shape[1:], tokens.dtype).at[target].set(tokens)
-    )
+    picks = (expert_row[:, None] == jnp.arange(experts, dtype=jnp.int32)[None, :]) & live_mask[:, None]
+    picks = picks.astype(jnp.bfloat16)
+    earlier = (position[None, :] < position[:, None]).astype(jnp.bfloat16)
+    before = jnp.dot(earlier, picks, preferred_element_type=jnp.float32)
+    slot_rank = jnp.sum(before * picks.astype(jnp.float32), axis=1).astype(jnp.int32)
+    target = expert_row * capacity + slot_rank
+    slot_ids = jnp.arange(experts * capacity, dtype=jnp.int32)
+    slot_hot = ((target[:, None] == slot_ids[None, :]) & live_mask[:, None]).astype(tokens.dtype)
+    buffer = lax.dot_general(
+        slot_hot, tokens, (((0,), (0,)), ((), ())), preferred_element_type=jnp.float32
+    ).astype(tokens.dtype)
     arrived = lax.all_to_all(
-        buffer[:-1].reshape((experts, capacity) + tokens.shape[1:]),
+        buffer.reshape((experts, capacity) + tokens.shape[1:]),
         "expert",
         split_axis=0,
         concat_axis=0,
@@ -81,10 +84,7 @@
         tiled=True,
     )
     flat_rows = returned.reshape((experts * capacity,) + returned.shape[2:])
-    padded = jnp.concatenate(
-        [flat_rows, jnp.zeros((1,) + flat_rows.shape[1:], flat_rows.dtype)], axis=0
-    )
-    return padded[target]
+    return jnp.dot(slot_hot, flat_rows, preferred_element_type=jnp.float32).astype(flat_rows.dtype)
 
 
 def solution(mesh):

time: 179 us -> 177 us (0.989)
  blocking collectives: 124 us -> 164 us
  waiting for transfers between devices: 30.7 us -> 0 us
  starting transfers between devices: 9.25 us -> 0 us
  local copies, waits for them, and re-layouts: 3.83 us -> 0.35 us
  matrix products: 5.56 us -> 8.51 us
  other arithmetic: 4.46 us -> 2.56 us
    all_to_all x1 -> x2, blocking collectives: 60.9 us -> 101 us  [the longest x1 60.9 us: per_device(): lax.all_to_all(buffer.reshape((experts, capacity) + tokens.shape[1:]), 'e...]
    all_to_all x1 -> x0, waiting for transfers between devices: 30.7 us -> none  [per_device(): lax.all_to_all(summed.reshape(arrived.shape[0], capacity, summed.shape[1]...]
    all_to_all x1 -> x0, starting transfers between devices: 9.25 us -> none  [per_device(): lax.all_to_all(summed.reshape(arrived.shape[0], capacity, summed.shape[1]...]
    dot_general x0 -> x3, matrix products: none -> 2.96 us  [the longest x1 1.13 us: per_device(): lax.dot_general(slot_hot, tokens, (((0,), (0,)), ((), ())), preferred_ele...]
  transfers between devices with their start and end apart: 1 -> 0, of which waited for: 1 -> 0; matrix products, arithmetic and copies ran while one was open for 0% -> 0% of each run, Pallas kernels for 0% -> 0%
where the time goes in v4:
time: 177 us; the launch traced here: 176 us
  blocking collectives  164 us (93%)
  matrix products  8.51 us (5%)
  other arithmetic  2.56 us (1%)
    all_to_all x1, blocking collectives, per_device(): lax.all_to_all(buffer.reshape((experts, capacity) + tokens.shape[1:]), 'e...  60.9 us
    all_to_all x1, blocking collectives, per_device(): lax.all_to_all(summed.reshape(arrived.shape[0], capacity, summed.shape[1]...  39.7 us
    all_to_all x1, blocking collectives, gather_mp(): return lax.all_to_all(copies, 'mp', split_axis=0, concat_axis=0, tiled=True)  33.5 us
    all_to_all x1, blocking collectives, reduce_scatter_mp(): lax.all_to_all(parts, 'mp', split_axis=0, concat_axis=0, tiled=True)  29.9 us
    dot_general x1, matrix products, per_device(): jnp.einsum('sf,jkf->jsk', hidden_grad, weight_blocks, preferred_element_t...  5.55 us

profile of v4, /device:TPU:1, one launch (start us, length us, event | category | flops | bytes accessed | tf_op | source)
XLA Modules:
  0.0 176.3 jit_solution(1198448935257939366)
XLA Ops:
  0.0 0.0 copy-start
  0.8 1.0 fusion
  1.8 0.7 fusion.28
  2.5 1.1 convolution_convert_fusion
  3.6 60.9 %all_to_all.20 = bf16[64,4,256]{2,1,0:T(4,128)(2,1)S(1)} all-to-all(bf16[64,4,256]{2,1,0:T(4,128)(2,1)S(1)} %reshape.50), channel_id=1, replica_groups=mesh['expert'=64,'mp'=16] {'expert'}, dimensions={0} | all-to-all | bytes 262144 | tf_op jit(solution)/shard_map/all_to_all | solution.py:57
  64.6 0.2 broadcast_in_dim.19
  64.8 0.0 copy-start.1
  64.8 33.5 %all_to_all.21 = bf16[16,256,256]{2,1,0:T(8,128)(2,1)} all-to-all(bf16[16,256,256]{2,1,0:T(8,128)(2,1)S(1)} %broadcast_in_dim.19), channel_id=1, replica_groups=mesh['expert'=64,'mp'=16] {'mp'}, dimensions={0} | all-to-all | bytes 4194304 | tf_op jit(solution)/shard_map/all_to_all | solution.py:22
  98.3 0.0 copy-done
  98.3 0.0 copy-done.1
  98.3 5.6 %convert_bitcast_fusion = bf16[16,256,256]{2,1,0:T(8,128)(2,1)} fusion(bf16[16,256,384]{2,1,0:T(8,128)(2,1)S(1)} %bitcast.35, bf16[16,256,256]{2,1,0:T(8,128)(2,1)} %all_to_all.21, bf16[1,256,384]{2,1,0:T(8,128)(2,1)S(1)} %copy-done.1), kind=kOutput, calls=%fused_computation | convolution fusion | flops 1613627392 | bytes 7536640 | tf_op jit(solution)/shard_map/sf,jkf->jsk/dot_general | solution.py:75
  103.8 29.9 %all_to_all.22 = bf16[16,256,256]{2,1,0:T(8,128)(2,1)} all-to-all(bf16[16,256,256]{2,1,0:T(8,128)(2,1)} %convert_bitcast_fusion), channel_id=1, replica_groups=mesh['expert'=64,'mp'=16] {'mp'}, dimensions={0} | all-to-all | bytes 4194304 | tf_op jit(solution)/shard_map/all_to_all | solution.py:26
  133.7 1.9 %reduce_sum.26 = bf16[256,256]{1,0:T(8,128)(2,1)S(1)} reduce(bf16[16,256,256]{2,1,0:T(8,128)(2,1)} %all_to_all.22, bf16[]{:T(256)} %constant.48.clone.1), dimensions={0}, to_apply=%region_1.2 | reduce | flops 983040 | bytes 2228226 | tf_op jit(solution)/shard_map/reduce_sum | solution.py:27
  135.7 39.7 %all_to_all.23 = bf16[64,4,256]{2,1,0:T(4,128)(2,1)S(1)} all-to-all(bf16[64,4,256]{2,1,0:T(4,128)(2,1)S(1)} %reshape.51), channel_id=1, replica_groups=mesh['expert'=64,'mp'=16] {'expert'}, dimensions={0} | all-to-all | bytes 262144 | tf_op jit(solution)/shard_map/all_to_all | solution.py:79
  175.4 0.9 convolution_convert_fusion.1
  (5 shorter events, 0.2 us)
Async XLA Ops:
  0.0 98.3 %copy-start = (bf16[1,4096,384]{2,1,0:T(8,128)(2,1)S(1)}, bf16[1,4096,384]{2,1,0:T(8,128)(2,1)}, u32[]{:S(2)}) copy-start(bf16[1,4096,384]{2,1,0:T(8,128)(2,1)} %param.9) | copy-start | bytes 9437188
  64.8 33.5 %copy-start.1 = (bf16[1,256,384]{2,1,0:T(8,128)(2,1)S(1)}, bf16[1,256,384]{2,1,0:T(8,128)(2,1)}, u32[]{:S(2)}) copy-start(bf16[1,256,384]{2,1,0:T(8,128)(2,1)} %param.8) | copy-start | bytes 589828

commit v5 on v4

--- a/solution.py
+++ b/solution.py
@@ -3,6 +3,8 @@
 import jax
 import jax.numpy as jnp
 from jax import lax
+from jax.experimental import pallas as pl
+from jax.experimental.pallas import tpu as pltpu
 from jax.sharding import PartitionSpec as P
 
 SEQ_LEN = 128
@@ -22,9 +24,64 @@
     return lax.all_to_all(copies, "mp", split_axis=0, concat_axis=0, tiled=True)
 
 
+def hidden_kernel(features_ref, weight_ref, cotangent_ref, out_ref):
+    n_blk, _, d_blk = features_ref.shape
+    pre_act = jnp.zeros((features_ref.shape[1], weight_ref.shape[1]), jnp.float32)
+    for j in range(n_blk):
+        pre_act = pre_act + jnp.dot(
+            features_ref[j], weight_ref[j * d_blk:(j + 1) * d_blk, :],
+            preferred_element_type=jnp.float32,
+        )
+    hidden_grad = (cotangent_ref[...].astype(jnp.float32) * gelu_slope(pre_act)).astype(
+        jnp.bfloat16
+    )
+    for j in range(n_blk):
+        out_ref[j] = lax.dot_general(
+            hidden_grad, weight_ref[j * d_blk:(j + 1) * d_blk, :],
+            (((1,), (1,)), ((), ())), preferred_element_type=jnp.float32,
+        ).astype(out_ref.dtype)
+
+
+def block_parts_of(features, weight, cotangent):
+    n_blk, slots, d_blk = features.shape
+    ff = weight.shape[1]
+    vmem = pl.BlockSpec(memory_space=pltpu.VMEM)
+    return pl.pallas_call(
+        hidden_kernel,
+        out_shape=jax.ShapeDtypeStruct((n_blk, slots, d_blk), jnp.bfloat16),
+        in_specs=[vmem, vmem, vmem],
+        out_specs=vmem,
+        cost_estimate=pl.CostEstimate(
+            flops=4 * slots * n_blk * d_blk * ff,
+            transcendentals=slots * ff,
+            bytes_accessed=2 * (2 * features.size + weight.size + cotangent.size),
+        ),
+    )(features, weight, cotangent)
+
+
+def sum_kernel(parts_ref, out_ref):
+    total = parts_ref[0].astype(jnp.float32)
+    for j in range(1, parts_ref.shape[0]):
+        total = total + parts_ref[j].astype(jnp.float32)
+    out_ref[...] = total.astype(out_ref.dtype)
+
+
+def sum_blocks(parts):
+    vmem = pl.BlockSpec(memory_space=pltpu.VMEM)
+    return pl.pallas_call(
+        sum_kernel,
+        out_shape=jax.ShapeDtypeStruct(parts.shape[1:], jnp.bfloat16),
+        in_specs=[vmem],
+        out_specs=vmem,
+        cost_estimate=pl.CostEstimate(
+            flops=parts.size, transcendentals=0, bytes_accessed=2 * parts.size + parts.size // 8
+        ),
+    )(parts)
+
+
 def reduce_scatter_mp(parts):
     arrived = lax.all_to_all(parts, "mp", split_axis=0, concat_axis=0, tiled=True)
-    return jnp.sum(arrived.astype(jnp.float32), axis=0)
+    return sum_blocks(arrived)
 
 
 def per_device(tokens, expert_ids, seq_lengths, hidden_cotangent, w_in):
@@ -64,17 +121,7 @@
     slot_count = arrived.shape[0] * capacity
     n_mp = lax.axis_size("mp")
     blocks = gather_mp(arrived.reshape(slot_count, arrived.shape[2]))
-    weight = w_in[0]
-    weight_blocks = weight.reshape((n_mp, weight.shape[0] // n_mp, weight.shape[1]))
-    pre_act = jnp.einsum(
-        "jsk,jkf->sf", blocks, weight_blocks, preferred_element_type=jnp.float32
-    )
-    hidden_grad = (hidden_cotangent[0].astype(jnp.float32) * gelu_slope(pre_act)).astype(
-        jnp.bfloat16
-    )
-    block_parts = jnp.einsum(
-        "sf,jkf->jsk", hidden_grad, weight_blocks, preferred_element_type=jnp.float32
-    ).astype(jnp.bfloat16)
+    block_parts = block_parts_of(blocks, w_in[0], hidden_cotangent[0])
     summed = reduce_scatter_mp(block_parts).astype(jnp.bfloat16)
     returned = lax.all_to_all(
         summed.reshape(arrived.shape[0], capacity, summed.shape[1]),

time: 177 us -> 178 us (level)
  Pallas kernels: 0 us -> 9.01 us
  matrix products: 8.51 us -> 2.04 us
  other arithmetic: 2.56 us -> 0.68 us
    pallas_call x0 -> x2, Pallas kernels: none -> 9.01 us  [the longest x1 6.51 us: block_parts_of(): pl.pallas_call(hidden_kernel, out_shape=jax.ShapeDtypeStruct((n_blk, slot...]
    dot_general x1 -> x0, matrix products: 5.55 us -> none  [per_device(): jnp.einsum('sf,jkf->jsk', hidden_grad, weight_blocks, preferred_element_t...]
    reduce_sum x1 -> x0, other arithmetic: 1.88 us -> none  [reduce_scatter_mp(): return jnp.sum(arrived.astype(jnp.float32), axis=0)]
where the time goes in v5:
time: 178 us
  blocking collectives  164 us (92%)
  Pallas kernels  9.01 us (5%)
  matrix products  2.04 us (1%)
    all_to_all x1, blocking collectives, per_device(): lax.all_to_all(buffer.reshape((experts, capacity) + tokens.shape[1:]), 'e...  60.9 us
    all_to_all x1, blocking collectives, per_device(): lax.all_to_all(summed.reshape(arrived.shape[0], capacity, summed.shape[1]...  39.7 us
    all_to_all x1, blocking collectives, gather_mp(): return lax.all_to_all(copies, 'mp', split_axis=0, concat_axis=0, tiled=True)  33.4 us
    all_to_all x1, blocking collectives, reduce_scatter_mp(): lax.all_to_all(parts, 'mp', split_axis=0, concat_axis=0, tiled=True)  29.9 us
    pallas_call x1, Pallas kernels, block_parts_of(): pl.pallas_call(hidden_kernel, out_shape=jax.ShapeDtypeStruct((n_blk, slot...  6.51 us

profile of v5, /device:TPU:1, one launch (start us, length us, event | category | flops | bytes accessed | tf_op | source)
XLA Modules:
  0.0 177.6 jit_solution(13644188038816914570)
XLA Ops:
  0.0 0.0 copy-start
  0.7 0.9 fusion
  1.6 0.7 fusion.14
  2.3 0.0 copy-done
  2.3 0.3 convolution_convert_fusion
  2.6 60.9 %all_to_all.20 = bf16[64,4,256]{2,1,0:T(4,128)(2,1)S(1)} all-to-all(bf16[64,4,256]{2,1,0:T(4,128)(2,1)S(1)} %reshape.48), channel_id=1, replica_groups=mesh['expert'=64,'mp'=16] {'expert'}, dimensions={0} | all-to-all | bytes 262144 | tf_op jit(solution)/shard_map/all_to_all | solution.py:114
  63.5 0.2 broadcast_in_dim.19
  63.7 33.4 %all_to_all.21.features_ref = bf16[16,256,256]{2,1,0:T(8,128)(2,1)} all-to-all(bf16[16,256,256]{2,1,0:T(8,128)(2,1)S(1)} %broadcast_in_dim.19), channel_id=1, replica_groups=mesh['expert'=64,'mp'=16] {'mp'}, dimensions={0} | all-to-all | bytes 4194304 | tf_op jit(solution)/shard_map/all_to_all | solution.py:24
  97.1 6.5 %shard_map.55 = bf16[16,256,256]{2,1,0:T(8,128)(2,1)} custom-call(bf16[16,256,256]{2,1,0:T(8,128)(2,1)} %all_to_all.21.features_ref, bf16[4096,384]{1,0:T(8,128)(2,1)} %bitcast.13, bf16[256,384]{1,0:T(8,128)(2,1)} %bitcast.14), custom_call_target="tpu_custom_call" | custom-call | flops 1610612736 | bytes 7536640 | tf_op jit(solution)/shard_map/pallas_call | solution.py:49
  103.6 29.9 %all_to_all.22.parts_ref = bf16[16,256,256]{2,1,0:T(8,128)(2,1)} all-to-all(bf16[16,256,256]{2,1,0:T(8,128)(2,1)} %shard_map.55), channel_id=1, replica_groups=mesh['expert'=64,'mp'=16] {'mp'}, dimensions={0} | all-to-all | bytes 4194304 | tf_op jit(solution)/shard_map/all_to_all | solution.py:83
  133.5 2.5 %shard_map.56 = bf16[256,256]{1,0:T(8,128)(2,1)} custom-call(bf16[16,256,256]{2,1,0:T(8,128)(2,1)} %all_to_all.22.parts_ref), custom_call_target="tpu_custom_call" | custom-call | flops 1048576 | bytes 2228224 | tf_op jit(solution)/shard_map/pallas_call | solution.py:71
  136.0 0.9 reshape.49
  137.0 39.7 %all_to_all.23 = bf16[64,4,256]{2,1,0:T(4,128)(2,1)S(1)} all-to-all(bf16[64,4,256]{2,1,0:T(4,128)(2,1)S(1)} %reshape.49), channel_id=1, replica_groups=mesh['expert'=64,'mp'=16] {'expert'}, dimensions={0} | all-to-all | bytes 262144 | tf_op jit(solution)/shard_map/all_to_all | solution.py:126
  176.7 0.9 convolution_convert_fusion.1
  (4 shorter events, 0.1 us)
Async XLA Ops:
  0.0 2.3 %copy-start = (bf16[128,256]{1,0:T(8,128)(2,1)S(1)}, bf16[128,256]{1,0:T(8,128)(2,1)}, u32[]{:S(2)}) copy-start(bf16[128,256]{1,0:T(8,128)(2,1)} %param.5) | copy-start | bytes 196612

commit v6 on v4

--- a/solution.py
+++ b/solution.py
@@ -3,6 +3,8 @@
 import jax
 import jax.numpy as jnp
 from jax import lax
+from jax.experimental import pallas as pl
+from jax.experimental.pallas import tpu as pltpu
 from jax.sharding import PartitionSpec as P
 
 SEQ_LEN = 128
@@ -20,6 +22,73 @@
     n_mp = lax.axis_size("mp")
     copies = jnp.broadcast_to(block[None], (n_mp,) + block.shape)
     return lax.all_to_all(copies, "mp", split_axis=0, concat_axis=0, tiled=True)
+
+
+def hidden_kernel(features_ref, weight_ref, cotangent_ref, out_ref, pre_ref, grad_ref, held_ref):
+    phase, step = pl.program_id(0), pl.program_id(1)
+    steps = pl.num_programs(1)
+    per_step, _, d_blk = features_ref.shape
+    rows = per_step * d_blk
+
+    @pl.when(phase == 0)
+    def _():
+        @pl.when(step == 0)
+        def _():
+            pre_ref[...] = jnp.zeros_like(pre_ref)
+
+        held_ref[pl.ds(pl.multiple_of(step * rows, rows), rows), :] = weight_ref[...]
+        acc = pre_ref[...]
+        for jj in range(per_step):
+            acc = acc + jnp.dot(
+                features_ref[jj], weight_ref[jj * d_blk:(jj + 1) * d_blk, :],
+                preferred_element_type=jnp.float32,
+            )
+        pre_ref[...] = acc
+
+        @pl.when(step == steps - 1)
+        def _():
+            grad_ref[...] = (
+                cotangent_ref[...].astype(jnp.float32) * gelu_slope(pre_ref[...])
+            ).astype(grad_ref.dtype)
+
+    @pl.when(phase == 1)
+    def _():
+        hidden_grad = grad_ref[...]
+        for jj in range(per_step):
+            start = pl.multiple_of(step * rows + jj * d_blk, d_blk)
+            out_ref[jj] = lax.dot_general(
+                hidden_grad, held_ref[pl.ds(start, d_blk), :],
+                (((1,), (1,)), ((), ())), preferred_element_type=jnp.float32,
+            ).astype(out_ref.dtype)
+
+
+def block_parts_of(features, weight, cotangent, steps=4):
+    n_blk, slots, d_blk = features.shape
+    d_model, ff = weight.shape
+    per_step = n_blk // steps
+    last = steps - 1
+    return pl.pallas_call(
+        hidden_kernel,
+        out_shape=jax.ShapeDtypeStruct((n_blk, slots, d_blk), jnp.bfloat16),
+        grid=(2, steps),
+        in_specs=[
+            pl.BlockSpec((per_step, slots, d_blk), lambda p, j: (j * (1 - p) + last * p, 0, 0)),
+            pl.BlockSpec((per_step * d_blk, ff), lambda p, j: (j * (1 - p) + last * p, 0)),
+            pl.BlockSpec((slots, ff), lambda p, j: (0, 0)),
+        ],
+        out_specs=pl.BlockSpec((per_step, slots, d_blk), lambda p, j: (j * p, 0, 0)),
+        scratch_shapes=[
+            pltpu.VMEM((slots, ff), jnp.float32),
+            pltpu.VMEM((slots, ff), jnp.bfloat16),
+            pltpu.VMEM((d_model, ff), jnp.bfloat16),
+        ],
+        compiler_params=pltpu.CompilerParams(dimension_semantics=("arbitrary", "arbitrary")),
+        cost_estimate=pl.CostEstimate(
+            flops=4 * slots * d_model * ff,
+            transcendentals=slots * ff,
+            bytes_accessed=2 * (2 * features.size + weight.size + cotangent.size),
+        ),
+    )(features, weight, cotangent)
 
 
 def reduce_scatter_mp(parts):
@@ -64,17 +133,7 @@
     slot_count = arrived.shape[0] * capacity
     n_mp = lax.axis_size("mp")
     blocks = gather_mp(arrived.reshape(slot_count, arrived.shape[2]))
-    weight = w_in[0]
-    weight_blocks = weight.reshape((n_mp, weight.shape[0] // n_mp, weight.shape[1]))
-    pre_act = jnp.einsum(
-        "jsk,jkf->sf", blocks, weight_blocks, preferred_element_type=jnp.float32
-    )
-    hidden_grad = (hidden_cotangent[0].astype(jnp.float32) * gelu_slope(pre_act)).astype(
-        jnp.bfloat16
-    )
-    block_parts = jnp.einsum(
-        "sf,jkf->jsk", hidden_grad, weight_blocks, preferred_element_type=jnp.float32
-    ).astype(jnp.bfloat16)
+    block_parts = block_parts_of(blocks, w_in[0], hidden_cotangent[0])
     summed = reduce_scatter_mp(block_parts).astype(jnp.bfloat16)
     returned = lax.all_to_all(
         summed.reshape(arrived.shape[0], capacity, summed.shape[1]),

time: 177 us -> 175 us (0.989)
  Pallas kernels: 0 us -> 7.75 us
  matrix products: 8.51 us -> 2.04 us
    pallas_call x0 -> x1, Pallas kernels: none -> 7.75 us  [block_parts_of(): pl.pallas_call(hidden_kernel, out_shape=jax.ShapeDtypeStruct((n_blk, slot...]
    dot_general x1 -> x0, matrix products: 5.55 us -> none  [per_device(): jnp.einsum('sf,jkf->jsk', hidden_grad, weight_blocks, preferred_element_t...]
where the time goes in v6:
time: 175 us
  blocking collectives  163 us (93%)
  Pallas kernels  7.75 us (4%)
  matrix products  2.04 us (1%)
    all_to_all x1, blocking collectives, per_device(): lax.all_to_all(buffer.reshape((experts, capacity) + tokens.shape[1:]), 'e...  60.9 us
    all_to_all x1, blocking collectives, per_device(): lax.all_to_all(summed.reshape(arrived.shape[0], capacity, summed.shape[1]...  39.7 us
    all_to_all x1, blocking collectives, gather_mp(): return lax.all_to_all(copies, 'mp', split_axis=0, concat_axis=0, tiled=True)  33.4 us
    all_to_all x1, blocking collectives, reduce_scatter_mp(): lax.all_to_all(parts, 'mp', split_axis=0, concat_axis=0, tiled=True)  29.1 us
    pallas_call x1, Pallas kernels, block_parts_of(): pl.pallas_call(hidden_kernel, out_shape=jax.ShapeDtypeStruct((n_blk, slot...  7.75 us

profile of v6, /device:TPU:1, one launch (start us, length us, event | category | flops | bytes accessed | tf_op | source)
XLA Modules:
  0.0 174.9 jit_solution(11266930489485891335)
XLA Ops:
  0.0 0.0 copy-start
  0.7 0.9 fusion
  1.6 0.7 fusion.14
  2.3 0.0 copy-done
  2.3 0.3 convolution_convert_fusion
  2.6 60.9 %all_to_all.20 = bf16[64,4,256]{2,1,0:T(4,128)(2,1)S(1)} all-to-all(bf16[64,4,256]{2,1,0:T(4,128)(2,1)S(1)} %reshape.48), channel_id=1, replica_groups=mesh['expert'=64,'mp'=16] {'expert'}, dimensions={0} | all-to-all | bytes 262144 | tf_op jit(solution)/shard_map/all_to_all | solution.py:126
  63.5 0.2 broadcast_in_dim.19
  63.7 33.4 %all_to_all.21.features_ref = bf16[16,256,256]{2,1,0:T(8,128)(2,1)} all-to-all(bf16[16,256,256]{2,1,0:T(8,128)(2,1)S(1)} %broadcast_in_dim.19), channel_id=1, replica_groups=mesh['expert'=64,'mp'=16] {'mp'}, dimensions={0} | all-to-all | bytes 4194304 | tf_op jit(solution)/shard_map/all_to_all | solution.py:24
  97.1 7.7 %shard_map.55 = bf16[16,256,256]{2,1,0:T(8,128)(2,1)} custom-call(bf16[16,256,256]{2,1,0:T(8,128)(2,1)} %all_to_all.21.features_ref, bf16[4096,384]{1,0:T(8,128)(2,1)} %bitcast.13, bf16[256,384]{1,0:T(8,128)(2,1)} %bitcast.14), custom_call_target="tpu_custom_call" | custom-call | flops 1610612736 | bytes 7536640 | tf_op jit(solution)/shard_map/pallas_call | solution.py:70
  104.8 29.1 %all_to_all.22 = bf16[16,256,256]{2,1,0:T(8,128)(2,1)S(1)} all-to-all(bf16[16,256,256]{2,1,0:T(8,128)(2,1)} %shard_map.55), channel_id=1, replica_groups=mesh['expert'=64,'mp'=16] {'mp'}, dimensions={0} | all-to-all | bytes 4194304 | tf_op jit(solution)/shard_map/all_to_all | solution.py:95
  134.0 0.3 reduce_sum.26
  134.3 39.7 %all_to_all.23 = bf16[64,4,256]{2,1,0:T(4,128)(2,1)S(1)} all-to-all(bf16[64,4,256]{2,1,0:T(4,128)(2,1)S(1)} %reshape.49), channel_id=1, replica_groups=mesh['expert'=64,'mp'=16] {'expert'}, dimensions={0} | all-to-all | bytes 262144 | tf_op jit(solution)/shard_map/all_to_all | solution.py:138
  174.1 0.9 convolution_convert_fusion.1
  (5 shorter events, 0.2 us)
Async XLA Ops:
  0.0 2.3 %copy-start = (bf16[128,256]{1,0:T(8,128)(2,1)S(1)}, bf16[128,256]{1,0:T(8,128)(2,1)}, u32[]{:S(2)}) copy-start(bf16[128,256]{1,0:T(8,128)(2,1)} %param.5) | copy-start | bytes 196612

commit v7 on v6

--- a/solution.py
+++ b/solution.py
@@ -62,7 +62,7 @@
             ).astype(out_ref.dtype)
 
 
-def block_parts_of(features, weight, cotangent, steps=4):
+def block_parts_of(features, weight, cotangent, steps=2):
     n_blk, slots, d_blk = features.shape
     d_model, ff = weight.shape
     per_step = n_blk // steps

time: 175 us -> 174 us (level)
  no operation moved by 1% of the time
where the time goes in v7:
time: 174 us
  blocking collectives  163 us (94%)
  Pallas kernels  6.38 us (4%)
  matrix products  2.04 us (1%)
    all_to_all x1, blocking collectives, per_device(): lax.all_to_all(buffer.reshape((experts, capacity) + tokens.shape[1:]), 'e...  60.9 us
    all_to_all x1, blocking collectives, per_device(): lax.all_to_all(summed.reshape(arrived.shape[0], capacity, summed.shape[1]...  39.7 us
    all_to_all x1, blocking collectives, gather_mp(): return lax.all_to_all(copies, 'mp', split_axis=0, concat_axis=0, tiled=True)  33.4 us
    all_to_all x1, blocking collectives, reduce_scatter_mp(): lax.all_to_all(parts, 'mp', split_axis=0, concat_axis=0, tiled=True)  29.1 us
    pallas_call x1, Pallas kernels, block_parts_of(): pl.pallas_call(hidden_kernel, out_shape=jax.ShapeDtypeStruct((n_blk, slot...  6.38 us

profile of v7, /device:TPU:1, one launch (start us, length us, event | category | flops | bytes accessed | tf_op | source)
XLA Modules:
  0.0 173.6 jit_solution(5332788208974360052)
XLA Ops:
  0.0 0.0 copy-start
  0.7 0.9 fusion
  1.6 0.7 fusion.14
  2.3 0.0 copy-done
  2.3 0.3 convolution_convert_fusion
  2.6 60.9 %all_to_all.20 = bf16[64,4,256]{2,1,0:T(4,128)(2,1)S(1)} all-to-all(bf16[64,4,256]{2,1,0:T(4,128)(2,1)S(1)} %reshape.48), channel_id=1, replica_groups=mesh['expert'=64,'mp'=16] {'expert'}, dimensions={0} | all-to-all | bytes 262144 | tf_op jit(solution)/shard_map/all_to_all | solution.py:126
  63.5 0.2 broadcast_in_dim.19
  63.7 33.4 %all_to_all.21.features_ref = bf16[16,256,256]{2,1,0:T(8,128)(2,1)} all-to-all(bf16[16,256,256]{2,1,0:T(8,128)(2,1)S(1)} %broadcast_in_dim.19), channel_id=1, replica_groups=mesh['expert'=64,'mp'=16] {'mp'}, dimensions={0} | all-to-all | bytes 4194304 | tf_op jit(solution)/shard_map/all_to_all | solution.py:24
  97.1 6.4 %shard_map.55 = bf16[16,256,256]{2,1,0:T(8,128)(2,1)} custom-call(bf16[16,256,256]{2,1,0:T(8,128)(2,1)} %all_to_all.21.features_ref, bf16[4096,384]{1,0:T(8,128)(2,1)} %bitcast.13, bf16[256,384]{1,0:T(8,128)(2,1)} %bitcast.14), custom_call_target="tpu_custom_call" | custom-call | flops 1610612736 | bytes 7536640 | tf_op jit(solution)/shard_map/pallas_call | solution.py:70
  103.5 29.1 %all_to_all.22 = bf16[16,256,256]{2,1,0:T(8,128)(2,1)S(1)} all-to-all(bf16[16,256,256]{2,1,0:T(8,128)(2,1)} %shard_map.55), channel_id=1, replica_groups=mesh['expert'=64,'mp'=16] {'mp'}, dimensions={0} | all-to-all | bytes 4194304 | tf_op jit(solution)/shard_map/all_to_all | solution.py:95
  132.6 0.3 reduce_sum.26
  132.9 39.7 %all_to_all.23 = bf16[64,4,256]{2,1,0:T(4,128)(2,1)S(1)} all-to-all(bf16[64,4,256]{2,1,0:T(4,128)(2,1)S(1)} %reshape.49), channel_id=1, replica_groups=mesh['expert'=64,'mp'=16] {'expert'}, dimensions={0} | all-to-all | bytes 262144 | tf_op jit(solution)/shard_map/all_to_all | solution.py:138
  172.7 0.9 convolution_convert_fusion.1
  (5 shorter events, 0.2 us)
Async XLA Ops:
  0.0 2.3 %copy-start = (bf16[128,256]{1,0:T(8,128)(2,1)S(1)}, bf16[128,256]{1,0:T(8,128)(2,1)}, u32[]{:S(2)}) copy-start(bf16[128,256]{1,0:T(8,128)(2,1)} %param.5) | copy-start | bytes 196612

commit v8 on v7

--- a/solution.py
+++ b/solution.py
@@ -112,11 +112,12 @@
     )
     live_mask = position % SEQ_LEN < seq_length
     expert_row = expert_ids[:, 0]
-    picks = (expert_row[:, None] == jnp.arange(experts, dtype=jnp.int32)[None, :]) & live_mask[:, None]
-    picks = picks.astype(jnp.bfloat16)
-    earlier = (position[None, :] < position[:, None]).astype(jnp.bfloat16)
-    before = jnp.dot(earlier, picks, preferred_element_type=jnp.float32)
-    slot_rank = jnp.sum(before * picks.astype(jnp.float32), axis=1).astype(jnp.int32)
+    same_before = (
+        (expert_row[None, :] == expert_row[:, None])
+        & live_mask[None, :]
+        & (position[None, :] < position[:, None])
+    )
+    slot_rank = jnp.sum(same_before.astype(jnp.int32), axis=1)
     target = expert_row * capacity + slot_rank
     slot_ids = jnp.arange(experts * capacity, dtype=jnp.int32)
     slot_hot = ((target[:, None] == slot_ids[None, :]) & live_mask[:, None]).astype(tokens.dtype)

time: 174 us -> 174 us (level)
  no operation moved by 1% of the time
where the time goes in v8:
time: 174 us
  blocking collectives  163 us (94%)
  Pallas kernels  6.38 us (4%)
  other arithmetic  1.86 us (1%)
    all_to_all x1, blocking collectives, per_device(): lax.all_to_all(buffer.reshape((experts, capacity) + tokens.shape[1:]), 'e...  60.9 us
    all_to_all x1, blocking collectives, per_device(): lax.all_to_all(summed.reshape(arrived.shape[0], capacity, summed.shape[1]...  39.7 us
    all_to_all x1, blocking collectives, gather_mp(): return lax.all_to_all(copies, 'mp', split_axis=0, concat_axis=0, tiled=True)  33.4 us
    all_to_all x1, blocking collectives, reduce_scatter_mp(): lax.all_to_all(parts, 'mp', split_axis=0, concat_axis=0, tiled=True)  29.1 us
    pallas_call x1, Pallas kernels, block_parts_of(): pl.pallas_call(hidden_kernel, out_shape=jax.ShapeDtypeStruct((n_blk, slot...  6.38 us

profile of v8, /device:TPU:1, one launch (start us, length us, event | category | flops | bytes accessed | tf_op | source)
XLA Modules:
  0.0 173.6 jit_solution(4162856016718499195)
XLA Ops:
  0.0 0.0 copy-start
  0.7 0.9 convert_reduce_fusion
  1.6 0.7 fusion.9
  2.3 0.0 copy-done
  2.3 0.3 convolution_convert_fusion
  2.6 60.9 %all_to_all.20 = bf16[64,4,256]{2,1,0:T(4,128)(2,1)S(1)} all-to-all(bf16[64,4,256]{2,1,0:T(4,128)(2,1)S(1)} %reshape.65), channel_id=1, replica_groups=mesh['expert'=64,'mp'=16] {'expert'}, dimensions={0} | all-to-all | bytes 262144 | tf_op jit(solution)/shard_map/all_to_all | solution.py:127
  63.5 0.2 broadcast_in_dim.30
  63.7 33.4 %all_to_all.21.features_ref = bf16[16,256,256]{2,1,0:T(8,128)(2,1)} all-to-all(bf16[16,256,256]{2,1,0:T(8,128)(2,1)S(1)} %broadcast_in_dim.30), channel_id=1, replica_groups=mesh['expert'=64,'mp'=16] {'mp'}, dimensions={0} | all-to-all | bytes 4194304 | tf_op jit(solution)/shard_map/all_to_all | solution.py:24
  97.1 6.4 %shard_map.55 = bf16[16,256,256]{2,1,0:T(8,128)(2,1)} custom-call(bf16[16,256,256]{2,1,0:T(8,128)(2,1)} %all_to_all.21.features_ref, bf16[4096,384]{1,0:T(8,128)(2,1)} %bitcast.13, bf16[256,384]{1,0:T(8,128)(2,1)} %bitcast.14), custom_call_target="tpu_custom_call" | custom-call | flops 1610612736 | bytes 7536640 | tf_op jit(solution)/shard_map/pallas_call | solution.py:70
  103.5 29.1 %all_to_all.22 = bf16[16,256,256]{2,1,0:T(8,128)(2,1)S(1)} all-to-all(bf16[16,256,256]{2,1,0:T(8,128)(2,1)} %shard_map.55), channel_id=1, replica_groups=mesh['expert'=64,'mp'=16] {'mp'}, dimensions={0} | all-to-all | bytes 4194304 | tf_op jit(solution)/shard_map/all_to_all | solution.py:95
  132.6 0.3 reduce_sum.29
  133.0 39.7 %all_to_all.23 = bf16[64,4,256]{2,1,0:T(4,128)(2,1)S(1)} all-to-all(bf16[64,4,256]{2,1,0:T(4,128)(2,1)S(1)} %reshape.66), channel_id=1, replica_groups=mesh['expert'=64,'mp'=16] {'expert'}, dimensions={0} | all-to-all | bytes 262144 | tf_op jit(solution)/shard_map/all_to_all | solution.py:139
  172.7 0.9 convolution_convert_fusion.1
  (5 shorter events, 0.2 us)
Async XLA Ops:
  0.0 2.3 %copy-start = (bf16[128,256]{1,0:T(8,128)(2,1)S(1)}, bf16[128,256]{1,0:T(8,128)(2,1)}, u32[]{:S(2)}) copy-start(bf16[128,256]{1,0:T(8,128)(2,1)} %param.5) | copy-start | bytes 196612

commit v9 on v8

--- a/solution.py
+++ b/solution.py
@@ -116,9 +116,9 @@
         (expert_row[None, :] == expert_row[:, None])
         & live_mask[None, :]
         & (position[None, :] < position[:, None])
-    )
-    slot_rank = jnp.sum(same_before.astype(jnp.int32), axis=1)
-    target = expert_row * capacity + slot_rank
+    ).astype(jnp.int32)
+    offset = jnp.where(position[None, :] == 0, expert_row[:, None] * capacity, 0)
+    target = jnp.sum(same_before + offset, axis=1)
     slot_ids = jnp.arange(experts * capacity, dtype=jnp.int32)
     slot_hot = ((target[:, None] == slot_ids[None, :]) & live_mask[:, None]).astype(tokens.dtype)
     buffer = lax.dot_general(

time: 174 us -> 174 us (level)
  no operation moved by 1% of the time
where the time goes in v9:
time: 174 us
  blocking collectives  163 us (94%)
  Pallas kernels  6.39 us (4%)
  other arithmetic  1.86 us (1%)
    all_to_all x1, blocking collectives, per_device(): lax.all_to_all(buffer.reshape((experts, capacity) + tokens.shape[1:]), 'e...  60.9 us
    all_to_all x1, blocking collectives, per_device(): lax.all_to_all(summed.reshape(arrived.shape[0], capacity, summed.shape[1]...  39.7 us
    all_to_all x1, blocking collectives, gather_mp(): return lax.all_to_all(copies, 'mp', split_axis=0, concat_axis=0, tiled=True)  33.4 us
    all_to_all x1, blocking collectives, reduce_scatter_mp(): lax.all_to_all(parts, 'mp', split_axis=0, concat_axis=0, tiled=True)  29.1 us
    pallas_call x1, Pallas kernels, block_parts_of(): pl.pallas_call(hidden_kernel, out_shape=jax.ShapeDtypeStruct((n_blk, slot...  6.39 us

profile of v9, /device:TPU:1, one launch (start us, length us, event | category | flops | bytes accessed | tf_op | source)
XLA Modules:
  0.0 173.6 jit_solution(8614952594694425060)
XLA Ops:
  0.0 0.0 copy-start
  0.7 0.7 multiply_bitcast_fusion
  1.4 0.9 add_reduce_fusion
  2.3 0.0 copy-done
  2.3 0.3 convolution_convert_fusion
  2.6 60.9 %all_to_all.20 = bf16[64,4,256]{2,1,0:T(4,128)(2,1)S(1)} all-to-all(bf16[64,4,256]{2,1,0:T(4,128)(2,1)S(1)} %reshape.70), channel_id=1, replica_groups=mesh['expert'=64,'mp'=16] {'expert'}, dimensions={0} | all-to-all | bytes 262144 | tf_op jit(solution)/shard_map/all_to_all | solution.py:127
  63.5 0.2 broadcast_in_dim.57
  63.7 33.4 %all_to_all.21.features_ref = bf16[16,256,256]{2,1,0:T(8,128)(2,1)} all-to-all(bf16[16,256,256]{2,1,0:T(8,128)(2,1)S(1)} %broadcast_in_dim.57), channel_id=1, replica_groups=mesh['expert'=64,'mp'=16] {'mp'}, dimensions={0} | all-to-all | bytes 4194304 | tf_op jit(solution)/shard_map/all_to_all | solution.py:24
  97.1 6.4 %shard_map.55 = bf16[16,256,256]{2,1,0:T(8,128)(2,1)} custom-call(bf16[16,256,256]{2,1,0:T(8,128)(2,1)} %all_to_all.21.features_ref, bf16[4096,384]{1,0:T(8,128)(2,1)} %bitcast.9, bf16[256,384]{1,0:T(8,128)(2,1)} %bitcast.10), custom_call_target="tpu_custom_call" | custom-call | flops 1610612736 | bytes 7536640 | tf_op jit(solution)/shard_map/pallas_call | solution.py:70
  103.5 29.1 %all_to_all.22 = bf16[16,256,256]{2,1,0:T(8,128)(2,1)S(1)} all-to-all(bf16[16,256,256]{2,1,0:T(8,128)(2,1)} %shard_map.55), channel_id=1, replica_groups=mesh['expert'=64,'mp'=16] {'mp'}, dimensions={0} | all-to-all | bytes 4194304 | tf_op jit(solution)/shard_map/all_to_all | solution.py:95
  132.6 0.3 reduce_sum.26
  133.0 39.7 %all_to_all.23 = bf16[64,4,256]{2,1,0:T(4,128)(2,1)S(1)} all-to-all(bf16[64,4,256]{2,1,0:T(4,128)(2,1)S(1)} %reshape.71), channel_id=1, replica_groups=mesh['expert'=64,'mp'=16] {'expert'}, dimensions={0} | all-to-all | bytes 262144 | tf_op jit(solution)/shard_map/all_to_all | solution.py:139
  172.7 0.9 convolution_convert_fusion.1
  (5 shorter events, 0.2 us)
Async XLA Ops:
  0.0 2.3 %copy-start = (bf16[128,256]{1,0:T(8,128)(2,1)S(1)}, bf16[128,256]{1,0:T(8,128)(2,1)}, u32[]{:S(2)}) copy-start(bf16[128,256]{1,0:T(8,128)(2,1)} %param.5) | copy-start | bytes 196612

commit v10 on v7

--- a/solution.py
+++ b/solution.py
@@ -1,4 +1,6 @@
 import math
+
+import numpy as np
 
 import jax
 import jax.numpy as jnp
@@ -116,9 +118,9 @@
     picks = picks.astype(jnp.bfloat16)
     earlier = (position[None, :] < position[:, None]).astype(jnp.bfloat16)
     before = jnp.dot(earlier, picks, preferred_element_type=jnp.float32)
-    slot_rank = jnp.sum(before * picks.astype(jnp.float32), axis=1).astype(jnp.int32)
-    target = expert_row * capacity + slot_rank
-    slot_ids = jnp.arange(experts * capacity, dtype=jnp.int32)
+    first_slot = jnp.asarray(np.arange(experts, dtype=np.float32) * capacity)
+    target = jnp.sum((before + first_slot[None, :]) * picks.astype(jnp.float32), axis=1)
+    slot_ids = jnp.asarray(np.arange(experts * capacity, dtype=np.float32))
     slot_hot = ((target[:, None] == slot_ids[None, :]) & live_mask[:, None]).astype(tokens.dtype)
     buffer = lax.dot_general(
         slot_hot, tokens, (((0,), (0,)), ((), ())), preferred_element_type=jnp.float32

time: 174 us -> 173 us (level)
  no operation moved by 1% of the time
where the time goes in v10:
time: 173 us
  blocking collectives  163 us (94%)
  Pallas kernels  6.38 us (4%)
  matrix products  2.05 us (1%)
    all_to_all x1, blocking collectives, per_device(): lax.all_to_all(buffer.reshape((experts, capacity) + tokens.shape[1:]), 'e...  60.9 us
    all_to_all x1, blocking collectives, per_device(): lax.all_to_all(summed.reshape(arrived.shape[0], capacity, summed.shape[1]...  39.7 us
    all_to_all x1, blocking collectives, gather_mp(): return lax.all_to_all(copies, 'mp', split_axis=0, concat_axis=0, tiled=True)  33.4 us
    all_to_all x1, blocking collectives, reduce_scatter_mp(): lax.all_to_all(parts, 'mp', split_axis=0, concat_axis=0, tiled=True)  29.1 us
    pallas_call x1, Pallas kernels, block_parts_of(): pl.pallas_call(hidden_kernel, out_shape=jax.ShapeDtypeStruct((n_blk, slot...  6.38 us

profile of v10, /device:TPU:1, one launch (start us, length us, event | category | flops | bytes accessed | tf_op | source)
XLA Modules:
  0.0 172.9 jit_solution(14229706814974419074)
XLA Ops:
  0.0 0.0 copy-start
  0.7 0.9 fusion.1
  1.6 0.0 copy-done
  1.6 0.3 convolution_convert_fusion
  2.0 60.9 %all_to_all.20 = bf16[64,4,256]{2,1,0:T(4,128)(2,1)S(1)} all-to-all(bf16[64,4,256]{2,1,0:T(4,128)(2,1)S(1)} %reshape.43), channel_id=1, replica_groups=mesh['expert'=64,'mp'=16] {'expert'}, dimensions={0} | all-to-all | bytes 262144 | tf_op jit(solution)/shard_map/all_to_all | solution.py:128
  62.9 0.2 broadcast_in_dim.19
  63.1 33.4 %all_to_all.21.features_ref = bf16[16,256,256]{2,1,0:T(8,128)(2,1)} all-to-all(bf16[16,256,256]{2,1,0:T(8,128)(2,1)S(1)} %broadcast_in_dim.19), channel_id=1, replica_groups=mesh['expert'=64,'mp'=16] {'mp'}, dimensions={0} | all-to-all | bytes 4194304 | tf_op jit(solution)/shard_map/all_to_all | solution.py:26
  96.4 6.4 %shard_map.73 = bf16[16,256,256]{2,1,0:T(8,128)(2,1)} custom-call(bf16[16,256,256]{2,1,0:T(8,128)(2,1)} %all_to_all.21.features_ref, bf16[4096,384]{1,0:T(8,128)(2,1)} %bitcast.7, bf16[256,384]{1,0:T(8,128)(2,1)} %bitcast.8), custom_call_target="tpu_custom_call" | custom-call | flops 1610612736 | bytes 7536640 | tf_op jit(solution)/shard_map/pallas_call | solution.py:72
  102.8 29.1 %all_to_all.22 = bf16[16,256,256]{2,1,0:T(8,128)(2,1)S(1)} all-to-all(bf16[16,256,256]{2,1,0:T(8,128)(2,1)} %shard_map.73), channel_id=1, replica_groups=mesh['expert'=64,'mp'=16] {'mp'}, dimensions={0} | all-to-all | bytes 4194304 | tf_op jit(solution)/shard_map/all_to_all | solution.py:97
  132.0 0.3 reduce_sum.26
  132.3 39.7 %all_to_all.23 = bf16[64,4,256]{2,1,0:T(4,128)(2,1)S(1)} all-to-all(bf16[64,4,256]{2,1,0:T(4,128)(2,1)S(1)} %reshape.44), channel_id=1, replica_groups=mesh['expert'=64,'mp'=16] {'expert'}, dimensions={0} | all-to-all | bytes 262144 | tf_op jit(solution)/shard_map/all_to_all | solution.py:140
  172.1 0.9 convolution_convert_fusion.1
  (5 shorter events, 0.2 us)
Async XLA Ops:
  0.0 1.6 copy-start
